TPU v7x, 256 devices: a whole 4x4x8 slice. The times are simulated.
256 devices in a mesh: seq: 64 (over x, z, core), ch: 4 (over y).
Axes of the slice: x: 4, y: 4, z: 8, core: 2. Of those that a mesh axis runs over, the one named last changes fastest.
Arguments:
- inputs: bfloat16 [8192, 4096], P('seq'), may hold values from -6 to 6
- norm_gain: float32 [4096], replicated, may hold values from 0.1 to 1.9
- in_weight: bfloat16 [4096, 3, 1024], P('seq', None, 'ch'), may hold values from -0.09375 to 0.09375
- short_filter: float32 [3, 3, 1024], P(None, None, 'ch'), may hold values from -4 to 4
- long_filter: float32 [8192, 1024], P('seq', 'ch'), may hold values from -2.2 to 2.2
- conv_bias: float32 [1024], P('ch'), may hold values from -4 to 4
- out_weight: bfloat16 [1024, 4096], P('ch', 'seq'), may hold values from -0.1875 to 0.1875
- out_grad: bfloat16 [8192, 4096], P('seq'), may hold values from -6 to 6
Outputs:
- block_out: bfloat16 [8192, 4096], P('seq', 'ch')
- in_grad: bfloat16 [8192, 4096], P('seq')
- filter_grad: float32 [8192, 1024], P('seq', 'ch')
All inputs are finite; a program needn't handle non-finite values.
Results may differ from a plain program's by a relative error of at most 0.013.
Values may be sent and summed in bfloat16 or wider, within the bound.
No kernel may reach another device: no remote copies, remote signals or barrier semaphores. Data moves between devices by JAX's collectives and lax.ppermute only.
A program may use at most 64 MiB of HBM per device.

v0:
```python
import math

import jax
import jax.numpy as jnp
from jax import lax
from jax.sharding import PartitionSpec as P

epsilon = 1e-05
highest = lax.Precision.HIGHEST


def passed_along(block, axis, distance):
    devices = range(lax.axis_size(axis))
    route = [(i - distance, i) for i in devices if i - distance in devices]
    return lax.ppermute(block, axis, route)


def doubled_gather(block, axis):
    devices = lax.axis_size(axis)
    place = lax.axis_index(axis)
    bits = devices.bit_length() - 1
    assert 1 << bits == devices
    gathered = block
    for bit in reversed(range(bits)):
        route = [(i, i ^ (1 << bit)) for i in range(devices)]
        arrived = lax.ppermute(gathered, axis, route)
        lower = ((place >> bit) & 1) == 0
        gathered = jnp.where(lower, jnp.stack([gathered, arrived]), jnp.stack([arrived, gathered]))
    gathered = gathered.transpose(tuple(reversed(range(bits))) + tuple(range(bits, gathered.ndim)))
    return gathered.reshape((devices * block.shape[0],) + block.shape[1:])


def halved_sum(partial, axis):
    devices = lax.axis_size(axis)
    place = lax.axis_index(axis)
    bits = devices.bit_length() - 1
    assert 1 << bits == devices
    rows, width = partial.shape
    share = width // devices
    held = partial.reshape((rows,) + (2,) * bits + (share,))
    held = held.transpose((0,) + tuple(range(bits, 0, -1)) + (bits + 1,)).astype(jnp.float32)
    for bit in range(bits):
        route = [(i, i ^ (1 << bit)) for i in range(devices)]
        mine = (place >> bit) & 1
        kept = lax.dynamic_index_in_dim(held, mine, 1, keepdims=False)
        given = lax.dynamic_index_in_dim(held, 1 - mine, 1, keepdims=False)
        arrived = lax.ppermute(given.astype(jnp.bfloat16), axis, route)
        held = kept + arrived.astype(jnp.float32)
    return held


def to_columns(signals):
    return lax.all_to_all(signals, "seq", split_axis=1, concat_axis=2, tiled=True)


def to_rows(signals):
    count, chans, seq_total = signals.shape
    devices = lax.axis_size("seq")
    local_rows = seq_total // devices
    pieces = signals.reshape(count, chans, devices, local_rows).transpose(2, 0, 1, 3)
    arrived = lax.all_to_all(pieces, "seq", split_axis=0, concat_axis=0, tiled=True)
    return arrived.transpose(1, 3, 0, 2).reshape(count, local_rows, devices * chans)


def turn_table(rows, cols, period, sign):
    turns = jnp.arange(rows, dtype=jnp.int32)[:, None] * jnp.arange(cols, dtype=jnp.int32)[None, :]
    turns = lax.optimization_barrier(turns)
    phases = sign * 2.0 * math.pi / period * (turns % period).astype(jnp.float32)
    return (jnp.cos(phases), jnp.sin(phases))


def fft_sizes(seq_total):
    total = 2 * seq_total
    inner = 1
    while inner * inner < total:
        inner *= 2
    return total // inner, inner


def forward_dft(signals):
    count, chans, seq_total = signals.shape
    outer, inner = fft_sizes(seq_total)
    grid = signals.reshape(count, chans, outer // 2, inner)
    cos_out, sin_out = turn_table(outer, outer // 2, outer, 1.0)
    first_real = jnp.einsum("kn,ucnm->uckm", cos_out, grid, precision=highest)
    first_imag = -jnp.einsum("kn,ucnm->uckm", sin_out, grid, precision=highest)
    cos_tw, sin_tw = turn_table(outer, inner, outer * inner, 1.0)
    turned_real = first_real * cos_tw + first_imag * sin_tw
    turned_imag = first_imag * cos_tw - first_real * sin_tw
    cos_in, sin_in = turn_table(inner, inner, inner, 1.0)
    spec_real = jnp.einsum("uckm,mj->uckj", turned_real, cos_in, precision=highest) + jnp.einsum(
        "uckm,mj->uckj", turned_imag, sin_in, precision=highest
    )
    spec_imag = jnp.einsum("uckm,mj->uckj", turned_imag, cos_in, precision=highest) - jnp.einsum(
        "uckm,mj->uckj", turned_real, sin_in, precision=highest
    )
    return spec_real, spec_imag


def inverse_dft(spec_real, spec_imag):
    count, chans, outer, inner = spec_real.shape
    cos_in, sin_in = turn_table(inner, inner, inner, 1.0)
    back_real = jnp.einsum("uckj,jm->uckm", spec_real, cos_in, precision=highest) - jnp.einsum(
        "uckj,jm->uckm", spec_imag, sin_in, precision=highest
    )
    back_imag = jnp.einsum("uckj,jm->uckm", spec_imag, cos_in, precision=highest) + jnp.einsum(
        "uckj,jm->uckm", spec_real, sin_in, precision=highest
    )
    cos_tw, sin_tw = turn_table(outer, inner, outer * inner, 1.0)
    turned_real = back_real * cos_tw - back_imag * sin_tw
    turned_imag = back_imag * cos_tw + back_real * sin_tw
    cos_out, sin_out = turn_table(outer, outer // 2, outer, 1.0)
    grid = jnp.einsum("kn,uckm->ucnm", cos_out, turned_real, precision=highest) - jnp.einsum(
        "kn,uckm->ucnm", sin_out, turned_imag, precision=highest
    )
    return grid.reshape(count, chans, outer * inner // 2) / float(outer * inner)


def per_device(
    inputs, norm_gain, in_weight, short_filter, long_filter, conv_bias, out_weight, out_grad
):
    local_rows = inputs.shape[0]
    model_width = inputs.shape[1]
    slab_width = long_filter.shape[1]
    taps = short_filter.shape[1]
    wide_inputs = inputs.astype(jnp.float32)
    inv_rms = lax.rsqrt(jnp.mean(wide_inputs * wide_inputs, axis=1, keepdims=True) + epsilon)
    normed = (wide_inputs * inv_rms * norm_gain).astype(jnp.bfloat16)
    in_panel, out_panel = (
        lax.all_gather(in_weight.reshape(in_weight.shape[0], -1), "seq", axis=0, tiled=True),
        doubled_gather(out_weight.T, "seq").T,
    )
    in_flat = in_panel.reshape(model_width, 3 * slab_width)
    projected = jnp.dot(normed, in_flat, preferred_element_type=jnp.float32)
    projected = projected.astype(jnp.bfloat16).reshape(local_rows, 3, slab_width)
    upper_rim = passed_along(projected[local_rows - (taps - 1) :], "seq", 1)
    extended = jnp.concatenate([upper_rim, projected], 0).astype(jnp.float32)
    mixed = jnp.zeros((local_rows, 3, slab_width), jnp.float32)
    for offset in range(taps):
        begin = taps - 1 - offset
        mixed = mixed + short_filter[:, offset, :][None] * extended[begin : begin + local_rows]
    query_br = mixed[:, 0]
    key_br = mixed[:, 1]
    value_br = mixed[:, 2]
    product = key_br * value_br
    gate_grad = jnp.dot(out_grad, out_panel.T, preferred_element_type=jnp.float32)
    carried = gate_grad * query_br
    filt_real, filt_imag = forward_dft(to_columns(long_filter.T[None]))
    filt_real, filt_imag = (filt_real[0], filt_imag[0])
    columns = to_columns(jnp.stack([product, carried]).transpose(0, 2, 1))
    all_real, all_imag = forward_dft(columns)
    sig_real, grad_real = (all_real[0], all_real[1])
    sig_imag, grad_imag = (all_imag[0], all_imag[1])
    conv_real = sig_real * filt_real - sig_imag * filt_imag
    conv_imag = sig_real * filt_imag + sig_imag * filt_real
    back_real = grad_real * filt_real + grad_imag * filt_imag
    back_imag = grad_imag * filt_real - grad_real * filt_imag
    pair_real = grad_real * sig_real + grad_imag * sig_imag
    pair_imag = grad_imag * sig_real - grad_real * sig_imag
    outs = inverse_dft(
        jnp.stack([conv_real, back_real, pair_real]), jnp.stack([conv_imag, back_imag, pair_imag])
    )
    returned = to_rows(outs)
    conv_out = returned[0]
    back_conv = returned[1]
    filter_grad = returned[2] * float(local_rows * lax.axis_size("seq")) ** (-0.5)
    biased = conv_out + conv_bias * product
    gated = (query_br * biased).astype(jnp.bfloat16)
    partial_out = jnp.dot(gated, out_panel, preferred_element_type=jnp.float32)
    source_grad = back_conv + conv_bias * carried
    mixed_grad = jnp.stack([gate_grad * biased, source_grad * value_br, source_grad * key_br], 1)
    lower_rim = passed_along(mixed_grad[: taps - 1], "seq", -1)
    extended_back = jnp.concatenate([mixed_grad, lower_rim], 0)
    proj_grad = jnp.zeros((local_rows, 3, slab_width), jnp.float32)
    for offset in range(taps):
        proj_grad = (
            proj_grad
            + short_filter[:, offset, :][None] * extended_back[offset : offset + local_rows]
        )
    proj_grad = proj_grad.astype(jnp.bfloat16).reshape(local_rows, 3 * slab_width)
    partial_grad = jnp.dot(proj_grad, in_flat.T, preferred_element_type=jnp.float32)
    ch_size = lax.axis_size("ch")
    feature_share = model_width // ch_size
    partial_inner = jnp.sum(partial_grad * (norm_gain * wide_inputs), axis=1, keepdims=True)
    inner_high = partial_inner.astype(jnp.bfloat16)
    inner_low = (partial_inner - inner_high.astype(jnp.float32)).astype(jnp.bfloat16)
    extra = jnp.concatenate(
        [inner_high, inner_low, jnp.zeros((local_rows, 126), jnp.bfloat16)], axis=1
    )
    payload = jnp.concatenate(
        [
            partial_out.astype(jnp.bfloat16).reshape(local_rows, ch_size, feature_share).transpose(1, 0, 2),
            partial_grad.astype(jnp.bfloat16).reshape(local_rows, ch_size, feature_share).transpose(1, 0, 2),
            jnp.broadcast_to(extra[None], (ch_size, local_rows, 128)),
        ],
        axis=2,
    )
    reduced = lax.psum_scatter(payload, "ch", scatter_dimension=0).astype(jnp.float32)
    summed = reduced[:, :feature_share]
    norm_grad = reduced[:, feature_share : 2 * feature_share]
    inner_at = 2 * feature_share
    inner_term = (reduced[:, inner_at : inner_at + 1] + reduced[:, inner_at + 1 : inner_at + 2]) / model_width
    feature_begin = lax.axis_index("ch") * feature_share
    residual = lax.dynamic_slice_in_dim(wide_inputs, feature_begin, feature_share, 1)
    block_out = (residual + summed).astype(jnp.bfloat16)
    gain_share = lax.dynamic_slice_in_dim(norm_gain, feature_begin, feature_share, 0)
    inputs_share = lax.dynamic_slice_in_dim(wide_inputs, feature_begin, feature_share, 1)
    grad_share = lax.dynamic_slice_in_dim(out_grad, feature_begin, feature_share, 1)
    weighted = norm_grad * gain_share
    in_grad_share = (
        grad_share.astype(jnp.float32) + weighted * inv_rms - inputs_share * inv_rms**3 * inner_term
    ).astype(jnp.bfloat16)
    in_grad = doubled_gather(in_grad_share[None], "ch").transpose(1, 0, 2).reshape(local_rows, model_width)
    return (block_out, in_grad, filter_grad)


def solution(mesh):
    return jax.shard_map(
        per_device,
        mesh=mesh,
        in_specs=(
            P("seq", None),
            P(),
            P("seq", None, "ch"),
            P(None, None, "ch"),
            P("seq", "ch"),
            P("ch"),
            P("ch", "seq"),
            P("seq", None),
        ),
        out_specs=(P("seq", "ch"), P("seq", None), P("seq", "ch")),
        check_vma=False,
    )
```

profile of v0, /device:TPU:2, one launch (start us, length us, event | category | flops | bytes accessed | tf_op | source)
XLA Modules:
  0.0 262.6 jit_solution(642104595003464655)
XLA Ops:
  8.8 2.2 collective-permute-start.1
  12.6 11.0 %all-to-all-start.1 = ((f32[1,256,128]{2,0,1:T(1,128)}), f32[1,256,128]{2,0,1:T(1,128)S(1)}, u32[]{:S(2)}, u32[]{:S(2)}) async-start(f32[1,256,128]{2,0,1:T(1,128)} %bitcast.46), calls=%async_computation.1 | async-start | bytes 262144 | tf_op jit(solution)/shard_map/all_to_all | solution.py:53
  27.0 3.9 %collective-permute-done.2 = bf16[2,64,256]{2,1,0:T(8,128)(2,1)S(1)} collective-permute-done((bf16[2,64,256]{2,1,0:T(8,128)(2,1)S(1)}, bf16[2,64,256]{2,1,0:T(8,128)(2,1)S(1)}, u32[]{:S(2)}, u32[]{:S(2)}) %collective-permute-start.2) | collective-permute-done | bytes 65568 | tf_op jit(solution)/shard_map/ppermute | solution.py:26
  31.0 5.3 %collective-permute-start.3 = (bf16[2,2,64,256]{3,2,0,1:T(8,128)(2,1)S(1)}, bf16[2,2,64,256]{3,2,0,1:T(8,128)(2,1)S(1)}, u32[]{:S(2)}, u32[]{:S(2)}) collective-permute-start(bf16[2,2,64,256]{3,2,0,1:T(8,128)(2,1)S(1)} %maximum_select_fusion.7), channel_id=1, source_target_pairs={{0,32},{4,36},{8,40},{12,44},{16,48},{20,52},{24,56},{28,60},{32,0... | collective-permute-start | bytes 393224 | tf_op jit(solution)/shard_map/ppermute | solution.py:26
  36.4 6.3 %collective-permute-done.3 = bf16[2,2,64,256]{3,2,0,1:T(8,128)(2,1)S(1)} collective-permute-done((bf16[2,2,64,256]{3,2,0,1:T(8,128)(2,1)S(1)}, bf16[2,2,64,256]{3,2,0,1:T(8,128)(2,1)S(1)}, u32[]{:S(2)}, u32[]{:S(2)}) %collective-permute-start.3) | collective-permute-done | bytes 131104 | tf_op jit(solution)/shard_map/ppermute | solution.py:26
  42.7 3.0 %collective-permute-start.4 = (bf16[2,2,2,64,256]{4,3,0,1,2:T(8,128)(2,1)S(1)}, bf16[2,2,2,64,256]{4,3,0,1,2:T(8,128)(2,1)S(1)}, u32[]{:S(2)}, u32[]{:S(2)}) collective-permute-start(bf16[2,2,2,64,256]{4,3,0,1,2:T(8,128)(2,1)S(1)} %maximum_select_fusion.6), channel_id=1, source_target_pairs={{0,16},{4,20},{8,24},{12,28},{16,0},{20,4},{24,8},{28,12},{32,48},... | collective-permute-start | bytes 786440 | tf_op jit(solution)/shard_map/ppermute | solution.py:26
  45.8 11.4 %collective-permute-done.4 = bf16[2,2,2,64,256]{4,3,0,1,2:T(8,128)(2,1)S(1)} collective-permute-done((bf16[2,2,2,64,256]{4,3,0,1,2:T(8,128)(2,1)S(1)}, bf16[2,2,2,64,256]{4,3,0,1,2:T(8,128)(2,1)S(1)}, u32[]{:S(2)}, u32[]{:S(2)}) %collective-permute-start.4) | collective-permute-done | bytes 262176 | tf_op jit(solution)/shard_map/ppermute | solution.py:26
  58.1 13.6 %collective-permute-done.5 = bf16[2,2,2,2,64,256]{5,4,0,1,2,3:T(8,128)(2,1)S(1)} collective-permute-done((bf16[2,2,2,2,64,256]{5,4,0,1,2,3:T(8,128)(2,1)S(1)}, bf16[2,2,2,2,64,256]{5,4,0,1,2,3:T(8,128)(2,1)S(1)}, u32[]{:S(2)}, u32[]{:S(2)}) %collective-permute-start.5) | collective-permute-done | bytes 524320 | tf_op jit(solution)/shard_map/ppermute | solution.py:26
  78.3 20.8 %all-gather.2.cloned.1.call-done = bf16[4096,768]{1,0:T(8,128)(2,1)} async-done(((bf16[64,768]{1,0:T(8,128)(2,1)}), bf16[4096,768]{1,0:T(8,128)(2,1)}) %all-gather.2.cloned.1.call-update) | async-done | bytes 6291472 | tf_op jit(solution)/shard_map/all_gather | solution.py:130
  99.1 3.9 %convolution_convert_fusion.1 = bf16[128,768]{1,0:T(8,128)(2,1)S(1)} fusion(bf16[4096,768]{1,0:T(8,128)(2,1)} %all-gather.2.cloned.1.call-done, bf16[128,4096]{1,0:T(8,128)(2,1)S(1)} %copy-done, f32[4096]{0:T(1024)} %param.9, f32[128]{0:T(128)S(1)} %get-tuple-element.42), kind=kOutput, calls=%fused_computation.15 | convolution fusion | flops 807501824 | bytes 7553536 | tf_op jit(solution)/shard_map/dot_general | solution.py:134
  104.3 2.1 collective-permute-start
  115.9 8.1 %all-to-all-start = ((f32[2,256,128]{2,0,1:T(2,128)}), f32[2,256,128]{2,0,1:T(2,128)}, u32[]{:S(2)}, u32[]{:S(2)}) async-start(f32[2,256,128]{2,0,1:T(2,128)} %copy.120), calls=%async_computation | async-start | bytes 524288 | tf_op jit(solution)/shard_map/all_to_all | solution.py:53
  125.7 2.3 fusion.3
  129.3 6.0 %all-to-all-done = f32[2,256,128]{2,0,1:T(2,128)} async-done(((f32[2,256,128]{2,0,1:T(2,128)}), f32[2,256,128]{2,0,1:T(2,128)}, u32[]{:S(2)}, u32[]{:S(2)}) %all-to-all-start) | async-done | bytes 262176 | tf_op jit(solution)/shard_map/all_to_all | solution.py:53
  135.3 2.0 fusion
  137.3 2.0 convolution_bitcast_fusion
  139.4 2.1 fusion.52
  152.8 6.7 %all-to-all-start.2 = ((f32[64,3,4,128]{3,2,1,0:T(4,128)}), f32[64,3,4,128]{3,2,1,0:T(4,128)}, u32[]{:S(2)}, u32[]{:S(2)}) async-start(f32[64,3,4,128]{3,2,1,0:T(4,128)} %copy.131), calls=%async_computation.2 | async-start | bytes 786432 | tf_op jit(solution)/shard_map/all_to_all | solution.py:61
  159.6 13.9 %all-to-all-done.2 = f32[64,3,4,128]{3,2,1,0:T(4,128)} async-done(((f32[64,3,4,128]{3,2,1,0:T(4,128)}), f32[64,3,4,128]{3,2,1,0:T(4,128)}, u32[]{:S(2)}, u32[]{:S(2)}) %all-to-all-start.2) | async-done | bytes 393248 | tf_op jit(solution)/shard_map/all_to_all | solution.py:61
  180.7 2.9 %collective-permute-start.7 = (f32[2,3,256]{2,0,1:T(2,128)S(1)}, f32[2,3,256]{2,0,1:T(2,128)S(1)}, u32[]{:S(2)}, u32[]{:S(2)}) collective-permute-start(f32[2,3,256]{2,0,1:T(2,128)S(1)} %slice.119), channel_id=1, source_target_pairs={{4,0},{8,4},{12,8},{16,12},{20,16},{24,20},{28,24},{32,28},{36,32}... | collective-permute-start | bytes 18440 | tf_op jit(solution)/shard_map/ppermute | solution.py:15
  186.2 5.0 %fusion.116 = (bf16[128,4096]{1,0:T(8,128)(2,1)S(1)}, f32[128]{0:T(128)S(1)}) fusion(bf16[128,4096]{1,0:T(8,128)(2,1)S(1)} %copy-done, f32[4096]{0:T(1024)S(1)} %copy-done.20, bf16[128,768]{0,1:T(8,128)(2,1)S(1)} %bitcast.260, bf16[4096,768]{1,0:T(8,128)(2,1)} %all-gather.2.cloned.1.call-done), kind=kOutput, calls=%fused_computation.190 | convolution fusion | flops 807927680 | bytes 8602112 | tf_op jit(solution)/shard_map/dot_general | solution.py:181
  196.3 31.6 %reduce-scatter.2.cloned.1.call-done = bf16[1,128,2176]{2,1,0:T(8,128)(2,1)} async-done(((bf16[4,128,2176]{2,1,0:T(8,128)(2,1)}), bf16[1,128,2176]{2,1,0:T(8,128)(2,1)}) %reduce-scatter.2.cloned.1.call-update) | async-done | bytes 557072 | tf_op jit(solution)/shard_map/reduce_scatter | solution.py:198
  232.6 8.0 %collective-permute-done.8 = bf16[1,128,1024]{2,1,0:T(8,128)(2,1)S(1)} collective-permute-done((bf16[1,128,1024]{2,1,0:T(8,128)(2,1)S(1)}, bf16[1,128,1024]{2,1,0:T(8,128)(2,1)S(1)}, u32[]{:S(2)}, u32[]{:S(2)}) %collective-permute-start.8) | collective-permute-done | bytes 262176 | tf_op jit(solution)/shard_map/ppermute | solution.py:26
  241.9 11.7 %collective-permute-done.9 = bf16[2,1,128,1024]{3,2,1,0:T(8,128)(2,1)S(1)} collective-permute-done((bf16[2,1,128,1024]{3,2,1,0:T(8,128)(2,1)S(1)}, bf16[2,1,128,1024]{3,2,1,0:T(8,128)(2,1)S(1)}, u32[]{:S(2)}, u32[]{:S(2)}) %collective-permute-start.9) | collective-permute-done | bytes 524320 | tf_op jit(solution)/shard_map/ppermute | solution.py:26
  (153 shorter events, 61.9 us)
Async XLA Ops:
  7.2 19.3 %copy-start.18 = (bf16[256,64]{0,1:T(8,128)(2,1)S(1)}, bf16[256,64]{0,1:T(8,128)(2,1)}, u32[]{:S(2)}) copy-start(bf16[256,64]{0,1:T(8,128)(2,1)} %param.14) | copy-start | bytes 98308
  7.2 91.9 %all-gather.2.cloned.1.call-start = ((), (), s32[]{:S(2)}) async-start(), calls=%async_computation.4 | async-start | bytes 6389760 | tf_op jit(solution)/shard_map/all_gather | solution.py:130
  8.8 17.6 %collective-permute-start.1 = (bf16[64,256]{1,0:T(8,128)(2,1)}, bf16[64,256]{1,0:T(8,128)(2,1)S(1)}, u32[]{:S(2)}, u32[]{:S(2)}) collective-permute-start(bf16[64,256]{1,0:T(8,128)(2,1)} %bitcast.267), channel_id=1, source_target_pairs={{0,128},{4,132},{8,136},{12,140},{16,144},{20,148},{24,152},{28,15... | collective-permute-start | bytes 98312 | tf_op jit(solution)/shard_map/ppermute | solution.py:26
  12.6 61.6 %all-to-all-start.1 = ((f32[1,256,128]{2,0,1:T(1,128)}), f32[1,256,128]{2,0,1:T(1,128)S(1)}, u32[]{:S(2)}, u32[]{:S(2)}) async-start(f32[1,256,128]{2,0,1:T(1,128)} %bitcast.46), calls=%async_computation.1 | async-start | bytes 262144 | tf_op jit(solution)/shard_map/all_to_all | solution.py:53
  24.8 48.7 %copy-start.4 = (f32[128,128]{1,0:T(8,128)}, f32[128,128]{1,0:T(8,128)S(1)}, u32[]{:S(2)}) copy-start(f32[128,128]{1,0:T(8,128)S(1)} %get-tuple-element.37) | copy-start | bytes 196612
  26.4 4.5 %collective-permute-start.2 = (bf16[2,64,256]{2,1,0:T(8,128)(2,1)S(1)}, bf16[2,64,256]{2,1,0:T(8,128)(2,1)S(1)}, u32[]{:S(2)}, u32[]{:S(2)}) collective-permute-start(bf16[2,64,256]{2,1,0:T(8,128)(2,1)S(1)} %maximum_select_fusion.8), channel_id=1, source_target_pairs={{0,64},{4,68},{8,72},{12,76},{16,80},{20,84},{24,88},{28,92},{32,9... | collective-permute-start | bytes 196616 | tf_op jit(solution)/shard_map/ppermute | solution.py:26
  31.0 11.7 %collective-permute-start.3 = (bf16[2,2,64,256]{3,2,0,1:T(8,128)(2,1)S(1)}, bf16[2,2,64,256]{3,2,0,1:T(8,128)(2,1)S(1)}, u32[]{:S(2)}, u32[]{:S(2)}) collective-permute-start(bf16[2,2,64,256]{3,2,0,1:T(8,128)(2,1)S(1)} %maximum_select_fusion.7), channel_id=1, source_target_pairs={{0,32},{4,36},{8,40},{12,44},{16,48},{20,52},{24,56},{28,60},{32,0... | collective-permute-start | bytes 393224 | tf_op jit(solution)/shard_map/ppermute | solution.py:26
  42.7 14.5 %collective-permute-start.4 = (bf16[2,2,2,64,256]{4,3,0,1,2:T(8,128)(2,1)S(1)}, bf16[2,2,2,64,256]{4,3,0,1,2:T(8,128)(2,1)S(1)}, u32[]{:S(2)}, u32[]{:S(2)}) collective-permute-start(bf16[2,2,2,64,256]{4,3,0,1,2:T(8,128)(2,1)S(1)} %maximum_select_fusion.6), channel_id=1, source_target_pairs={{0,16},{4,20},{8,24},{12,28},{16,0},{20,4},{24,8},{28,12},{32,48},... | collective-permute-start | bytes 786440 | tf_op jit(solution)/shard_map/ppermute | solution.py:26
  57.3 14.4 %collective-permute-start.5 = (bf16[2,2,2,2,64,256]{5,4,0,1,2,3:T(8,128)(2,1)S(1)}, bf16[2,2,2,2,64,256]{5,4,0,1,2,3:T(8,128)(2,1)S(1)}, u32[]{:S(2)}, u32[]{:S(2)}) collective-permute-start(bf16[2,2,2,2,64,256]{5,4,0,1,2,3:T(8,128)(2,1)S(1)} %maximum_select_fusion.3), channel_id=1, source_target_pairs={{0,8},{4,12},{8,0},{12,4},{16,24},{20,28},{24,16},{28,20},{32,40},... | collective-permute-start | bytes 1572872 | tf_op jit(solution)/shard_map/ppermute | solution.py:26
  58.0 41.1 %copy-start.23 = (f32[128]{0:T(128)}, f32[128]{0:T(128)S(1)}, u32[]{:S(2)}) copy-start(f32[128]{0:T(128)S(1)} %get-tuple-element.42) | copy-start | bytes 1540
  72.8 3.6 %collective-permute-start.6 = (bf16[2,2,2,2,2,64,256]{6,5,0,1,2,3,4:T(8,128)(2,1)}, bf16[2,2,2,2,2,64,256]{6,5,0,1,2,3,4:T(8,128)(2,1)}, u32[]{:S(2)}, u32[]{:S(2)}) collective-permute-start(bf16[2,2,2,2,2,64,256]{6,5,0,1,2,3,4:T(8,128)(2,1)} %maximum_select_fusion.1), channel_id=1, source_target_pairs={{0,4},{4,0},{8,12},{12,8},{16,20},{20,16},{24,28},{28,24},{32,36},... | collective-permute-start | bytes 3145736 | tf_op jit(solution)/shard_map/ppermute | solution.py:26
  76.4 22.7 %copy-start = (bf16[128,4096]{1,0:T(8,128)(2,1)S(1)}, bf16[128,4096]{1,0:T(8,128)(2,1)}, u32[]{:S(2)}) copy-start(bf16[128,4096]{1,0:T(8,128)(2,1)} %param.8) | copy-start | bytes 3145732
  104.3 7.2 %collective-permute-start = (bf16[2,3,256]{2,0,1:T(2,128)(2,1)}, bf16[2,3,256]{2,0,1:T(2,128)(2,1)S(1)}, u32[]{:S(2)}, u32[]{:S(2)}) collective-permute-start(bf16[2,3,256]{2,0,1:T(2,128)(2,1)} %bitcast), channel_id=1, source_target_pairs={{0,4},{4,8},{8,12},{12,16},{16,20},{20,24},{24,28},{28,32},{32,36}... | collective-permute-start | bytes 9224 | tf_op jit(solution)/shard_map/ppermute | solution.py:15
  115.9 19.4 %all-to-all-start = ((f32[2,256,128]{2,0,1:T(2,128)}), f32[2,256,128]{2,0,1:T(2,128)}, u32[]{:S(2)}, u32[]{:S(2)}) async-start(f32[2,256,128]{2,0,1:T(2,128)} %copy.120), calls=%async_computation | async-start | bytes 524288 | tf_op jit(solution)/shard_map/all_to_all | solution.py:53
  151.8 26.7 %copy-start.13 = (f32[128,256]{1,0:T(8,128)S(1)}, f32[128,256]{1,0:T(8,128)}, u32[]{:S(2)}) copy-start(f32[128,256]{1,0:T(8,128)} %convolution_bitcast_fusion.2) | copy-start | bytes 393220
  151.8 26.7 %copy-start.21 = (f32[256]{0:T(256)S(1)}, f32[256]{0:T(256)}, u32[]{:S(2)}) copy-start(f32[256]{0:T(256)} %param.13) | copy-start | bytes 3076
  152.8 20.7 %all-to-all-start.2 = ((f32[64,3,4,128]{3,2,1,0:T(4,128)}), f32[64,3,4,128]{3,2,1,0:T(4,128)}, u32[]{:S(2)}, u32[]{:S(2)}) async-start(f32[64,3,4,128]{3,2,1,0:T(4,128)} %copy.131), calls=%async_computation.2 | async-start | bytes 786432 | tf_op jit(solution)/shard_map/all_to_all | solution.py:61
  159.5 68.4 %reduce-scatter.2.cloned.1.call-start = ((), (), s32[]{:S(2)}) async-start(), calls=%async_computation.5 | async-start | bytes 2785280 | tf_op jit(solution)/shard_map/reduce_scatter | solution.py:198
  180.7 4.8 %collective-permute-start.7 = (f32[2,3,256]{2,0,1:T(2,128)S(1)}, f32[2,3,256]{2,0,1:T(2,128)S(1)}, u32[]{:S(2)}, u32[]{:S(2)}) collective-permute-start(f32[2,3,256]{2,0,1:T(2,128)S(1)} %slice.119), channel_id=1, source_target_pairs={{4,0},{8,4},{12,8},{16,12},{20,16},{24,20},{28,24},{32,28},{36,32}... | collective-permute-start | bytes 18440 | tf_op jit(solution)/shard_map/ppermute | solution.py:15
  196.0 33.2 %copy-start.22 = (f32[128]{0:T(128)S(1)}, f32[128]{0:T(128)}, u32[]{:S(2)}) copy-start(f32[128]{0:T(128)} %get-tuple-element.41) | copy-start | bytes 1540
  196.0 33.2 %copy-start.24 = (f32[128]{0:T(128)S(1)}, f32[128]{0:T(128)}, u32[]{:S(2)}) copy-start(f32[128]{0:T(128)} %copy-done.23) | copy-start | bytes 1540
  229.0 12.0 %copy-start.17 = (f32[1,128,64,4]{1,3,0,2:T(4,128)S(1)}, f32[1,128,64,4]{1,3,0,2:T(4,128)}, u32[]{:S(2)}) copy-start(f32[1,128,64,4]{1,3,0,2:T(4,128)} %get-tuple-element.29) | copy-start | bytes 393220
  231.1 9.5 %collective-permute-start.8 = (bf16[1,128,1024]{2,1,0:T(8,128)(2,1)S(1)}, bf16[1,128,1024]{2,1,0:T(8,128)(2,1)S(1)}, u32[]{:S(2)}, u32[]{:S(2)}) collective-permute-start(bf16[1,128,1024]{2,1,0:T(8,128)(2,1)S(1)} %bitcast.245), channel_id=1, source_target_pairs={{0,2},{1,3},{2,0},{3,1},{4,6},{5,7},{6,4},{7,5},{8,10},{9,11},{10,... | collective-permute-start | bytes 786440 | tf_op jit(solution)/shard_map/ppermute | solution.py:26
  240.7 12.8 %collective-permute-start.9 = (bf16[2,1,128,1024]{3,2,1,0:T(8,128)(2,1)S(1)}, bf16[2,1,128,1024]{3,2,1,0:T(8,128)(2,1)S(1)}, u32[]{:S(2)}, u32[]{:S(2)}) collective-permute-start(bf16[2,1,128,1024]{3,2,1,0:T(8,128)(2,1)S(1)} %maximum_select_fusion.5), channel_id=1, source_target_pairs={{0,1},{1,0},{2,3},{3,2},{4,5},{5,4},{6,7},{7,6},{8,9},{9,8},{10,11... | collective-permute-start | bytes 1572872 | tf_op jit(solution)/shard_map/ppermute | solution.py:26
  (16 other events, 54.3 us)
Sparse Core Ops, SparseCore 0:
  10.7 88.3 all-gather.1
  196.2 31.6 reduce-scatter.1
where the time goes:
time: 264 us; the launch traced here: 263 us
  waiting for transfers between devices  128 us (48%)
  starting transfers between devices  43.8 us (17%)
  matrix products  35.3 us (13%)
  local copies, waits for them, and re-layouts  23.5 us (9%)
  other arithmetic  17.5 us (7%)
  between operations  14.8 us (6%)
    ppermute x8, waiting for transfers between devices, doubled_gather(): arrived = lax.ppermute(gathered, axis, route)  55 us
    reduce_scatter x1, waiting for transfers between devices, per_device(): lax.psum_scatter(payload, 'ch', scatter_dimension=0).astype(jnp.float32)  31.6 us
    all_gather x1, waiting for transfers between devices, per_device(): lax.all_gather(in_weight.reshape(in_weight.shape[0], -1), 'seq', axis=0,...  20.8 us
    all_to_all x2, starting transfers between devices, to_columns(): lax.all_to_all(signals, 'seq', split_axis=1, concat_axis=2, tiled=True)  19.1 us
    all_to_all x1, waiting for transfers between devices, to_rows(): lax.all_to_all(pieces, 'seq', split_axis=0, concat_axis=0, tiled=True)  13.9 us
    ppermute x8, starting transfers between devices, doubled_gather(): arrived = lax.ppermute(gathered, axis, route)  12.9 us
    all_to_all x1, starting transfers between devices, to_rows(): lax.all_to_all(pieces, 'seq', split_axis=0, concat_axis=0, tiled=True)  6.66 us
    all_to_all x2, waiting for transfers between devices, to_columns(): lax.all_to_all(signals, 'seq', split_axis=1, concat_axis=2, tiled=True)  5.98 us
  transfers between devices with their start and end apart: 15, of which 11 were waited for; matrix products, arithmetic and copies ran while one was open for 9% of the time, Pallas kernels for 0%

commit v1 on v0

--- a/solution.py
+++ b/solution.py
@@ -47,6 +47,18 @@
         arrived = lax.ppermute(given.astype(jnp.bfloat16), axis, route)
         held = kept + arrived.astype(jnp.float32)
     return held
+
+
+def ring_gather(block, axis):
+    devices = lax.axis_size(axis)
+    place = lax.axis_index(axis)
+    arrived = [block] + [
+        lax.ppermute(block, axis, [(i, (i + shift) % devices) for i in range(devices)])
+        for shift in range(1, devices)
+    ]
+    flipped = jnp.stack([arrived[(devices - m) % devices] for m in range(devices)])
+    doubled = jnp.concatenate([flipped, flipped], 0)
+    return lax.dynamic_slice_in_dim(doubled, (devices - place) % devices, devices, 0)
 
 
 def to_columns(signals):
@@ -210,7 +222,7 @@
     in_grad_share = (
         grad_share.astype(jnp.float32) + weighted * inv_rms - inputs_share * inv_rms**3 * inner_term
     ).astype(jnp.bfloat16)
-    in_grad = doubled_gather(in_grad_share[None], "ch").transpose(1, 0, 2).reshape(local_rows, model_width)
+    in_grad = ring_gather(in_grad_share, "ch").transpose(1, 0, 2).reshape(local_rows, model_width)
     return (block_out, in_grad, filter_grad)
 
 

time: 264 us -> 266 us (level)
  waiting for transfers between devices: 128 us -> 119 us
  local copies, waits for them, and re-layouts: 23.5 us -> 31.7 us
    ppermute x8 -> x6, waiting for transfers between devices: 55 us -> 35.3 us  [doubled_gather(): arrived = lax.ppermute(gathered, axis, route)]
    ppermute x0 -> x3, waiting for transfers between devices: none -> 10.8 us  [ring_gather(): lax.ppermute(block, axis, [(i, (i + shift) % devices) for i in range(devi...]
    unnamed x55 -> x59, local copies, waits for them, and re-layouts: 5.49 us -> 11.7 us
    ppermute x0 -> x3, starting transfers between devices: none -> 2.85 us  [ring_gather(): lax.ppermute(block, axis, [(i, (i + shift) % devices) for i in range(devi...]
    ppermute x8 -> x6, starting transfers between devices: 12.9 us -> 11.2 us  [doubled_gather(): arrived = lax.ppermute(gathered, axis, route)]
  transfers between devices with their start and end apart: 15 -> 16, of which waited for: 11 -> 12; matrix products, arithmetic and copies ran while one was open for 9% -> 11% of each run, Pallas kernels for 0% -> 0%
where the time goes in v1:
time: 266 us; the launch traced here: 263 us
  waiting for transfers between devices  119 us (45%)
  starting transfers between devices  44.9 us (17%)
  matrix products  35.3 us (13%)
  local copies, waits for them, and re-layouts  31.7 us (12%)
  other arithmetic  17.9 us (7%)
  between operations  14.8 us (6%)
    ppermute x6, waiting for transfers between devices, doubled_gather(): arrived = lax.ppermute(gathered, axis, route)  35.3 us
    reduce_scatter x1, waiting for transfers between devices, per_device(): lax.psum_scatter(payload, 'ch', scatter_dimension=0).astype(jnp.float32)  31.6 us
    all_gather x1, waiting for transfers between devices, per_device(): lax.all_gather(in_weight.reshape(in_weight.shape[0], -1), 'seq', axis=0,...  20.8 us
    all_to_all x2, starting transfers between devices, to_columns(): lax.all_to_all(signals, 'seq', split_axis=1, concat_axis=2, tiled=True)  19.1 us
    all_to_all x1, waiting for transfers between devices, to_rows(): lax.all_to_all(pieces, 'seq', split_axis=0, concat_axis=0, tiled=True)  13.9 us
    unnamed x59, local copies, waits for them, and re-layouts  11.7 us
    ppermute x6, starting transfers between devices, doubled_gather(): arrived = lax.ppermute(gathered, axis, route)  11.2 us
    ppermute x3, waiting for transfers between devices, ring_gather(): lax.ppermute(block, axis, [(i, (i + shift) % devices) for i in range(devi...  10.8 us
  transfers between devices with their start and end apart: 16, of which 12 were waited for; matrix products, arithmetic and copies ran while one was open for 11% of the time, Pallas kernels for 0%

profile of v1, /device:TPU:2, one launch (start us, length us, event | category | flops | bytes accessed | tf_op | source)
XLA Modules:
  0.0 263.4 jit_solution(2066496797926977343)
XLA Ops:
  8.8 2.2 collective-permute-start.1
  12.6 11.0 %all-to-all-start.1 = ((f32[1,256,128]{2,0,1:T(1,128)}), f32[1,256,128]{2,0,1:T(1,128)S(1)}, u32[]{:S(2)}, u32[]{:S(2)}) async-start(f32[1,256,128]{2,0,1:T(1,128)} %bitcast.46), calls=%async_computation.1 | async-start | bytes 262144 | tf_op jit(solution)/shard_map/all_to_all | solution.py:65
  27.0 3.9 %collective-permute-done.2 = bf16[2,64,256]{2,1,0:T(8,128)(2,1)S(1)} collective-permute-done((bf16[2,64,256]{2,1,0:T(8,128)(2,1)S(1)}, bf16[2,64,256]{2,1,0:T(8,128)(2,1)S(1)}, u32[]{:S(2)}, u32[]{:S(2)}) %collective-permute-start.2) | collective-permute-done | bytes 65568 | tf_op jit(solution)/shard_map/ppermute | solution.py:26
  31.0 5.3 %collective-permute-start.3 = (bf16[2,2,64,256]{3,2,0,1:T(8,128)(2,1)S(1)}, bf16[2,2,64,256]{3,2,0,1:T(8,128)(2,1)S(1)}, u32[]{:S(2)}, u32[]{:S(2)}) collective-permute-start(bf16[2,2,64,256]{3,2,0,1:T(8,128)(2,1)S(1)} %maximum_select_fusion.4), channel_id=1, source_target_pairs={{0,32},{4,36},{8,40},{12,44},{16,48},{20,52},{24,56},{28,60},{32,0... | collective-permute-start | bytes 393224 | tf_op jit(solution)/shard_map/ppermute | solution.py:26
  36.4 6.3 %collective-permute-done.3 = bf16[2,2,64,256]{3,2,0,1:T(8,128)(2,1)S(1)} collective-permute-done((bf16[2,2,64,256]{3,2,0,1:T(8,128)(2,1)S(1)}, bf16[2,2,64,256]{3,2,0,1:T(8,128)(2,1)S(1)}, u32[]{:S(2)}, u32[]{:S(2)}) %collective-permute-start.3) | collective-permute-done | bytes 131104 | tf_op jit(solution)/shard_map/ppermute | solution.py:26
  42.7 3.0 %collective-permute-start.4 = (bf16[2,2,2,64,256]{4,3,0,1,2:T(8,128)(2,1)S(1)}, bf16[2,2,2,64,256]{4,3,0,1,2:T(8,128)(2,1)S(1)}, u32[]{:S(2)}, u32[]{:S(2)}) collective-permute-start(bf16[2,2,2,64,256]{4,3,0,1,2:T(8,128)(2,1)S(1)} %maximum_select_fusion.3), channel_id=1, source_target_pairs={{0,16},{4,20},{8,24},{12,28},{16,0},{20,4},{24,8},{28,12},{32,48},... | collective-permute-start | bytes 786440 | tf_op jit(solution)/shard_map/ppermute | solution.py:26
  45.8 11.4 %collective-permute-done.4 = bf16[2,2,2,64,256]{4,3,0,1,2:T(8,128)(2,1)S(1)} collective-permute-done((bf16[2,2,2,64,256]{4,3,0,1,2:T(8,128)(2,1)S(1)}, bf16[2,2,2,64,256]{4,3,0,1,2:T(8,128)(2,1)S(1)}, u32[]{:S(2)}, u32[]{:S(2)}) %collective-permute-start.4) | collective-permute-done | bytes 262176 | tf_op jit(solution)/shard_map/ppermute | solution.py:26
  58.1 13.6 %collective-permute-done.5 = bf16[2,2,2,2,64,256]{5,4,0,1,2,3:T(8,128)(2,1)S(1)} collective-permute-done((bf16[2,2,2,2,64,256]{5,4,0,1,2,3:T(8,128)(2,1)S(1)}, bf16[2,2,2,2,64,256]{5,4,0,1,2,3:T(8,128)(2,1)S(1)}, u32[]{:S(2)}, u32[]{:S(2)}) %collective-permute-start.5) | collective-permute-done | bytes 524320 | tf_op jit(solution)/shard_map/ppermute | solution.py:26
  78.3 20.8 %all-gather.2.cloned.1.call-done = bf16[4096,768]{1,0:T(8,128)(2,1)} async-done(((bf16[64,768]{1,0:T(8,128)(2,1)}), bf16[4096,768]{1,0:T(8,128)(2,1)}) %all-gather.2.cloned.1.call-update) | async-done | bytes 6291472 | tf_op jit(solution)/shard_map/all_gather | solution.py:142
  99.1 3.9 %convolution_convert_fusion.1 = bf16[128,768]{1,0:T(8,128)(2,1)S(1)} fusion(bf16[4096,768]{1,0:T(8,128)(2,1)} %all-gather.2.cloned.1.call-done, bf16[128,4096]{1,0:T(8,128)(2,1)S(1)} %copy-done, f32[4096]{0:T(1024)} %param.9, f32[128]{0:T(128)S(1)} %get-tuple-element.39), kind=kOutput, calls=%fused_computation.15 | convolution fusion | flops 807501824 | bytes 7553536 | tf_op jit(solution)/shard_map/dot_general | solution.py:146
  104.3 2.1 collective-permute-start
  115.9 8.1 %all-to-all-start = ((f32[2,256,128]{2,0,1:T(2,128)}), f32[2,256,128]{2,0,1:T(2,128)}, u32[]{:S(2)}, u32[]{:S(2)}) async-start(f32[2,256,128]{2,0,1:T(2,128)} %copy.80), calls=%async_computation | async-start | bytes 524288 | tf_op jit(solution)/shard_map/all_to_all | solution.py:65
  125.7 2.3 fusion.3
  129.3 6.0 %all-to-all-done = f32[2,256,128]{2,0,1:T(2,128)} async-done(((f32[2,256,128]{2,0,1:T(2,128)}), f32[2,256,128]{2,0,1:T(2,128)}, u32[]{:S(2)}, u32[]{:S(2)}) %all-to-all-start) | async-done | bytes 262176 | tf_op jit(solution)/shard_map/all_to_all | solution.py:65
  135.3 2.0 fusion
  139.4 2.1 fusion.50
  152.8 6.7 %all-to-all-start.2 = ((f32[64,3,4,128]{3,2,1,0:T(4,128)}), f32[64,3,4,128]{3,2,1,0:T(4,128)}, u32[]{:S(2)}, u32[]{:S(2)}) async-start(f32[64,3,4,128]{3,2,1,0:T(4,128)} %copy.91), calls=%async_computation.2 | async-start | bytes 786432 | tf_op jit(solution)/shard_map/all_to_all | solution.py:73
  159.6 13.9 %all-to-all-done.2 = f32[64,3,4,128]{3,2,1,0:T(4,128)} async-done(((f32[64,3,4,128]{3,2,1,0:T(4,128)}), f32[64,3,4,128]{3,2,1,0:T(4,128)}, u32[]{:S(2)}, u32[]{:S(2)}) %all-to-all-start.2) | async-done | bytes 393248 | tf_op jit(solution)/shard_map/all_to_all | solution.py:73
  180.7 2.9 %collective-permute-start.7 = (f32[2,3,256]{2,0,1:T(2,128)S(1)}, f32[2,3,256]{2,0,1:T(2,128)S(1)}, u32[]{:S(2)}, u32[]{:S(2)}) collective-permute-start(f32[2,3,256]{2,0,1:T(2,128)S(1)} %slice.119), channel_id=1, source_target_pairs={{4,0},{8,4},{12,8},{16,12},{20,16},{24,20},{28,24},{32,28},{36,32}... | collective-permute-start | bytes 18440 | tf_op jit(solution)/shard_map/ppermute | solution.py:15
  186.2 5.0 %fusion.115 = (bf16[128,4096]{1,0:T(8,128)(2,1)S(1)}, f32[128]{0:T(128)S(1)}) fusion(bf16[128,4096]{1,0:T(8,128)(2,1)S(1)} %copy-done, f32[4096]{0:T(1024)S(1)} %copy-done.19, bf16[128,768]{0,1:T(8,128)(2,1)S(1)} %bitcast.257, bf16[4096,768]{1,0:T(8,128)(2,1)} %all-gather.2.cloned.1.call-done), kind=kOutput, calls=%fused_computation.194 | convolution fusion | flops 807927680 | bytes 8602112 | tf_op jit(solution)/shard_map/dot_general | solution.py:193
  196.3 31.6 %reduce-scatter.2.cloned.1.call-done = bf16[1,128,2176]{2,1,0:T(8,128)(2,1)} async-done(((bf16[4,128,2176]{2,1,0:T(8,128)(2,1)}), bf16[1,128,2176]{2,1,0:T(8,128)(2,1)}) %reduce-scatter.2.cloned.1.call-update) | async-done | bytes 557072 | tf_op jit(solution)/shard_map/reduce_scatter | solution.py:210
  236.4 4.1 %collective-permute-done.8 = bf16[128,1024]{1,0:T(8,128)(2,1)S(1)} collective-permute-done((bf16[128,1024]{1,0:T(8,128)(2,1)}, bf16[128,1024]{1,0:T(8,128)(2,1)S(1)}, u32[]{:S(2)}, u32[]{:S(2)}) %collective-permute-start.8) | collective-permute-done | bytes 262176 | tf_op jit(solution)/shard_map/ppermute | solution.py:56
  241.3 3.3 %collective-permute-done.9 = bf16[128,1024]{1,0:T(8,128)(2,1)S(1)} collective-permute-done((bf16[128,1024]{1,0:T(8,128)(2,1)}, bf16[128,1024]{1,0:T(8,128)(2,1)S(1)}, u32[]{:S(2)}, u32[]{:S(2)}) %collective-permute-start.9) | collective-permute-done | bytes 262176 | tf_op jit(solution)/shard_map/ppermute | solution.py:56
  245.3 3.3 %collective-permute-done.10 = bf16[128,1024]{1,0:T(8,128)(2,1)S(1)} collective-permute-done((bf16[128,1024]{1,0:T(8,128)(2,1)}, bf16[128,1024]{1,0:T(8,128)(2,1)S(1)}, u32[]{:S(2)}, u32[]{:S(2)}) %collective-permute-start.10) | collective-permute-done | bytes 262176 | tf_op jit(solution)/shard_map/ppermute | solution.py:56
  (158 shorter events, 73.6 us)
Async XLA Ops:
  7.2 19.3 %copy-start.17 = (bf16[256,64]{0,1:T(8,128)(2,1)S(1)}, bf16[256,64]{0,1:T(8,128)(2,1)}, u32[]{:S(2)}) copy-start(bf16[256,64]{0,1:T(8,128)(2,1)} %param.14) | copy-start | bytes 98308
  7.2 91.9 %all-gather.2.cloned.1.call-start = ((), (), s32[]{:S(2)}) async-start(), calls=%async_computation.4 | async-start | bytes 6389760 | tf_op jit(solution)/shard_map/all_gather | solution.py:142
  8.8 17.6 %collective-permute-start.1 = (bf16[64,256]{1,0:T(8,128)(2,1)}, bf16[64,256]{1,0:T(8,128)(2,1)S(1)}, u32[]{:S(2)}, u32[]{:S(2)}) collective-permute-start(bf16[64,256]{1,0:T(8,128)(2,1)} %bitcast.263), channel_id=1, source_target_pairs={{0,128},{4,132},{8,136},{12,140},{16,144},{20,148},{24,152},{28,15... | collective-permute-start | bytes 98312 | tf_op jit(solution)/shard_map/ppermute | solution.py:26
  12.6 61.6 %all-to-all-start.1 = ((f32[1,256,128]{2,0,1:T(1,128)}), f32[1,256,128]{2,0,1:T(1,128)S(1)}, u32[]{:S(2)}, u32[]{:S(2)}) async-start(f32[1,256,128]{2,0,1:T(1,128)} %bitcast.46), calls=%async_computation.1 | async-start | bytes 262144 | tf_op jit(solution)/shard_map/all_to_all | solution.py:65
  24.8 48.7 %copy-start.4 = (f32[128,128]{1,0:T(8,128)}, f32[128,128]{1,0:T(8,128)S(1)}, u32[]{:S(2)}) copy-start(f32[128,128]{1,0:T(8,128)S(1)} %get-tuple-element.34) | copy-start | bytes 196612
  26.4 4.5 %collective-permute-start.2 = (bf16[2,64,256]{2,1,0:T(8,128)(2,1)S(1)}, bf16[2,64,256]{2,1,0:T(8,128)(2,1)S(1)}, u32[]{:S(2)}, u32[]{:S(2)}) collective-permute-start(bf16[2,64,256]{2,1,0:T(8,128)(2,1)S(1)} %maximum_select_fusion.5), channel_id=1, source_target_pairs={{0,64},{4,68},{8,72},{12,76},{16,80},{20,84},{24,88},{28,92},{32,9... | collective-permute-start | bytes 196616 | tf_op jit(solution)/shard_map/ppermute | solution.py:26
  31.0 11.7 %collective-permute-start.3 = (bf16[2,2,64,256]{3,2,0,1:T(8,128)(2,1)S(1)}, bf16[2,2,64,256]{3,2,0,1:T(8,128)(2,1)S(1)}, u32[]{:S(2)}, u32[]{:S(2)}) collective-permute-start(bf16[2,2,64,256]{3,2,0,1:T(8,128)(2,1)S(1)} %maximum_select_fusion.4), channel_id=1, source_target_pairs={{0,32},{4,36},{8,40},{12,44},{16,48},{20,52},{24,56},{28,60},{32,0... | collective-permute-start | bytes 393224 | tf_op jit(solution)/shard_map/ppermute | solution.py:26
  42.7 14.5 %collective-permute-start.4 = (bf16[2,2,2,64,256]{4,3,0,1,2:T(8,128)(2,1)S(1)}, bf16[2,2,2,64,256]{4,3,0,1,2:T(8,128)(2,1)S(1)}, u32[]{:S(2)}, u32[]{:S(2)}) collective-permute-start(bf16[2,2,2,64,256]{4,3,0,1,2:T(8,128)(2,1)S(1)} %maximum_select_fusion.3), channel_id=1, source_target_pairs={{0,16},{4,20},{8,24},{12,28},{16,0},{20,4},{24,8},{28,12},{32,48},... | collective-permute-start | bytes 786440 | tf_op jit(solution)/shard_map/ppermute | solution.py:26
  57.3 14.4 %collective-permute-start.5 = (bf16[2,2,2,2,64,256]{5,4,0,1,2,3:T(8,128)(2,1)S(1)}, bf16[2,2,2,2,64,256]{5,4,0,1,2,3:T(8,128)(2,1)S(1)}, u32[]{:S(2)}, u32[]{:S(2)}) collective-permute-start(bf16[2,2,2,2,64,256]{5,4,0,1,2,3:T(8,128)(2,1)S(1)} %maximum_select_fusion.2), channel_id=1, source_target_pairs={{0,8},{4,12},{8,0},{12,4},{16,24},{20,28},{24,16},{28,20},{32,40},... | collective-permute-start | bytes 1572872 | tf_op jit(solution)/shard_map/ppermute | solution.py:26
  58.0 41.1 %copy-start.22 = (f32[128]{0:T(128)}, f32[128]{0:T(128)S(1)}, u32[]{:S(2)}) copy-start(f32[128]{0:T(128)S(1)} %get-tuple-element.39) | copy-start | bytes 1540
  72.8 3.6 %collective-permute-start.6 = (bf16[2,2,2,2,2,64,256]{6,5,0,1,2,3,4:T(8,128)(2,1)}, bf16[2,2,2,2,2,64,256]{6,5,0,1,2,3,4:T(8,128)(2,1)}, u32[]{:S(2)}, u32[]{:S(2)}) collective-permute-start(bf16[2,2,2,2,2,64,256]{6,5,0,1,2,3,4:T(8,128)(2,1)} %maximum_select_fusion.1), channel_id=1, source_target_pairs={{0,4},{4,0},{8,12},{12,8},{16,20},{20,16},{24,28},{28,24},{32,36},... | collective-permute-start | bytes 3145736 | tf_op jit(solution)/shard_map/ppermute | solution.py:26
  76.4 22.7 %copy-start = (bf16[128,4096]{1,0:T(8,128)(2,1)S(1)}, bf16[128,4096]{1,0:T(8,128)(2,1)}, u32[]{:S(2)}) copy-start(bf16[128,4096]{1,0:T(8,128)(2,1)} %param.8) | copy-start | bytes 3145732
  104.3 7.2 %collective-permute-start = (bf16[2,3,256]{2,0,1:T(2,128)(2,1)}, bf16[2,3,256]{2,0,1:T(2,128)(2,1)S(1)}, u32[]{:S(2)}, u32[]{:S(2)}) collective-permute-start(bf16[2,3,256]{2,0,1:T(2,128)(2,1)} %bitcast), channel_id=1, source_target_pairs={{0,4},{4,8},{8,12},{12,16},{16,20},{20,24},{24,28},{28,32},{32,36}... | collective-permute-start | bytes 9224 | tf_op jit(solution)/shard_map/ppermute | solution.py:15
  115.9 19.4 %all-to-all-start = ((f32[2,256,128]{2,0,1:T(2,128)}), f32[2,256,128]{2,0,1:T(2,128)}, u32[]{:S(2)}, u32[]{:S(2)}) async-start(f32[2,256,128]{2,0,1:T(2,128)} %copy.80), calls=%async_computation | async-start | bytes 524288 | tf_op jit(solution)/shard_map/all_to_all | solution.py:65
  151.8 26.7 %copy-start.13 = (f32[128,256]{1,0:T(8,128)S(1)}, f32[128,256]{1,0:T(8,128)}, u32[]{:S(2)}) copy-start(f32[128,256]{1,0:T(8,128)} %convolution_bitcast_fusion.2) | copy-start | bytes 393220
  151.8 26.7 %copy-start.20 = (f32[256]{0:T(256)S(1)}, f32[256]{0:T(256)}, u32[]{:S(2)}) copy-start(f32[256]{0:T(256)} %param.13) | copy-start | bytes 3076
  152.8 20.7 %all-to-all-start.2 = ((f32[64,3,4,128]{3,2,1,0:T(4,128)}), f32[64,3,4,128]{3,2,1,0:T(4,128)}, u32[]{:S(2)}, u32[]{:S(2)}) async-start(f32[64,3,4,128]{3,2,1,0:T(4,128)} %copy.91), calls=%async_computation.2 | async-start | bytes 786432 | tf_op jit(solution)/shard_map/all_to_all | solution.py:73
  159.5 68.4 %reduce-scatter.2.cloned.1.call-start = ((), (), s32[]{:S(2)}) async-start(), calls=%async_computation.5 | async-start | bytes 2785280 | tf_op jit(solution)/shard_map/reduce_scatter | solution.py:210
  180.7 4.8 %collective-permute-start.7 = (f32[2,3,256]{2,0,1:T(2,128)S(1)}, f32[2,3,256]{2,0,1:T(2,128)S(1)}, u32[]{:S(2)}, u32[]{:S(2)}) collective-permute-start(f32[2,3,256]{2,0,1:T(2,128)S(1)} %slice.119), channel_id=1, source_target_pairs={{4,0},{8,4},{12,8},{16,12},{20,16},{24,20},{28,24},{32,28},{36,32}... | collective-permute-start | bytes 18440 | tf_op jit(solution)/shard_map/ppermute | solution.py:15
  196.0 33.2 %copy-start.21 = (f32[128]{0:T(128)S(1)}, f32[128]{0:T(128)}, u32[]{:S(2)}) copy-start(f32[128]{0:T(128)} %get-tuple-element.38) | copy-start | bytes 1540
  196.0 33.2 %copy-start.23 = (f32[128]{0:T(128)S(1)}, f32[128]{0:T(128)}, u32[]{:S(2)}) copy-start(f32[128]{0:T(128)} %copy-done.22) | copy-start | bytes 1540
  231.2 9.4 %collective-permute-start.8 = (bf16[128,1024]{1,0:T(8,128)(2,1)}, bf16[128,1024]{1,0:T(8,128)(2,1)S(1)}, u32[]{:S(2)}, u32[]{:S(2)}) collective-permute-start(bf16[128,1024]{1,0:T(8,128)(2,1)} %get-tuple-element.10), channel_id=1, source_target_pairs={{0,3},{1,0},{2,1},{3,2},{4,7},{5,4},{6,5},{7,6},{8,11},{9,8},{10,9... | collective-permute-start | bytes 786440 | tf_op jit(solution)/shard_map/ppermute | solution.py:56
  233.7 10.9 %collective-permute-start.9 = (bf16[128,1024]{1,0:T(8,128)(2,1)}, bf16[128,1024]{1,0:T(8,128)(2,1)S(1)}, u32[]{:S(2)}, u32[]{:S(2)}) collective-permute-start(bf16[128,1024]{1,0:T(8,128)(2,1)} %get-tuple-element.10), channel_id=1, source_target_pairs={{0,2},{1,3},{2,0},{3,1},{4,6},{5,7},{6,4},{7,5},{8,10},{9,11},{10,... | collective-permute-start | bytes 786440 | tf_op jit(solution)/shard_map/ppermute | solution.py:56
  235.1 13.6 %collective-permute-start.10 = (bf16[128,1024]{1,0:T(8,128)(2,1)}, bf16[128,1024]{1,0:T(8,128)(2,1)S(1)}, u32[]{:S(2)}, u32[]{:S(2)}) collective-permute-start(bf16[128,1024]{1,0:T(8,128)(2,1)} %get-tuple-element.10), channel_id=1, source_target_pairs={{0,1},{1,2},{2,3},{3,0},{4,5},{5,6},{6,7},{7,4},{8,9},{9,10},{10,1... | collective-permute-start | bytes 786440 | tf_op jit(solution)/shard_map/ppermute | solution.py:56
  (16 other events, 54.3 us)
Sparse Core Ops, SparseCore 0:
  10.7 88.3 all-gather.1
  196.2 31.6 reduce-scatter.1

commit v2 on v0

--- a/solution.py
+++ b/solution.py
@@ -82,17 +82,17 @@
     outer, inner = fft_sizes(seq_total)
     grid = signals.reshape(count, chans, outer // 2, inner)
     cos_out, sin_out = turn_table(outer, outer // 2, outer, 1.0)
-    first_real = jnp.einsum("kn,ucnm->uckm", cos_out, grid, precision=highest)
-    first_imag = -jnp.einsum("kn,ucnm->uckm", sin_out, grid, precision=highest)
+    first_real = jnp.einsum("kn,ucnm->uckm", cos_out, grid, precision=lax.Precision.HIGH)
+    first_imag = -jnp.einsum("kn,ucnm->uckm", sin_out, grid, precision=lax.Precision.HIGH)
     cos_tw, sin_tw = turn_table(outer, inner, outer * inner, 1.0)
     turned_real = first_real * cos_tw + first_imag * sin_tw
     turned_imag = first_imag * cos_tw - first_real * sin_tw
     cos_in, sin_in = turn_table(inner, inner, inner, 1.0)
-    spec_real = jnp.einsum("uckm,mj->uckj", turned_real, cos_in, precision=highest) + jnp.einsum(
-        "uckm,mj->uckj", turned_imag, sin_in, precision=highest
-    )
-    spec_imag = jnp.einsum("uckm,mj->uckj", turned_imag, cos_in, precision=highest) - jnp.einsum(
-        "uckm,mj->uckj", turned_real, sin_in, precision=highest
+    spec_real = jnp.einsum("uckm,mj->uckj", turned_real, cos_in, precision=lax.Precision.HIGH) + jnp.einsum(
+        "uckm,mj->uckj", turned_imag, sin_in, precision=lax.Precision.HIGH
+    )
+    spec_imag = jnp.einsum("uckm,mj->uckj", turned_imag, cos_in, precision=lax.Precision.HIGH) - jnp.einsum(
+        "uckm,mj->uckj", turned_real, sin_in, precision=lax.Precision.HIGH
     )
     return spec_real, spec_imag
 
@@ -100,18 +100,18 @@
 def inverse_dft(spec_real, spec_imag):
     count, chans, outer, inner = spec_real.shape
     cos_in, sin_in = turn_table(inner, inner, inner, 1.0)
-    back_real = jnp.einsum("uckj,jm->uckm", spec_real, cos_in, precision=highest) - jnp.einsum(
-        "uckj,jm->uckm", spec_imag, sin_in, precision=highest
-    )
-    back_imag = jnp.einsum("uckj,jm->uckm", spec_imag, cos_in, precision=highest) + jnp.einsum(
-        "uckj,jm->uckm", spec_real, sin_in, precision=highest
+    back_real = jnp.einsum("uckj,jm->uckm", spec_real, cos_in, precision=lax.Precision.HIGH) - jnp.einsum(
+        "uckj,jm->uckm", spec_imag, sin_in, precision=lax.Precision.HIGH
+    )
+    back_imag = jnp.einsum("uckj,jm->uckm", spec_imag, cos_in, precision=lax.Precision.HIGH) + jnp.einsum(
+        "uckj,jm->uckm", spec_real, sin_in, precision=lax.Precision.HIGH
     )
     cos_tw, sin_tw = turn_table(outer, inner, outer * inner, 1.0)
     turned_real = back_real * cos_tw - back_imag * sin_tw
     turned_imag = back_imag * cos_tw + back_real * sin_tw
     cos_out, sin_out = turn_table(outer, outer // 2, outer, 1.0)
-    grid = jnp.einsum("kn,uckm->ucnm", cos_out, turned_real, precision=highest) - jnp.einsum(
-        "kn,uckm->ucnm", sin_out, turned_imag, precision=highest
+    grid = jnp.einsum("kn,uckm->ucnm", cos_out, turned_real, precision=lax.Precision.HIGH) - jnp.einsum(
+        "kn,uckm->ucnm", sin_out, turned_imag, precision=lax.Precision.HIGH
     )
     return grid.reshape(count, chans, outer * inner // 2) / float(outer * inner)
 

time: 264 us -> 259 us (0.981)
  matrix products: 35.3 us -> 30.3 us
    dot_general x18, matrix products: 23.3 us -> 18.3 us  [the longest x2 3.17 us: forward_dft(): jnp.einsum('uckm,mj->uckj', turned_real, cos_in, precision=lax.Precision....]
  transfers between devices with their start and end apart: 15 -> 15, of which waited for: 11 -> 12; matrix products, arithmetic and copies ran while one was open for 9% -> 9% of each run, Pallas kernels for 0% -> 0%
where the time goes in v2:
time: 259 us; the launch traced here: 258 us
  waiting for transfers between devices  128 us (49%)
  starting transfers between devices  43.8 us (17%)
  matrix products  30.3 us (12%)
  local copies, waits for them, and re-layouts  23.5 us (9%)
  other arithmetic  17.5 us (7%)
  between operations  14.8 us (6%)
    ppermute x8, waiting for transfers between devices, doubled_gather(): arrived = lax.ppermute(gathered, axis, route)  55.2 us
    reduce_scatter x1, waiting for transfers between devices, per_device(): lax.psum_scatter(payload, 'ch', scatter_dimension=0).astype(jnp.float32)  31.6 us
    all_gather x1, waiting for transfers between devices, per_device(): lax.all_gather(in_weight.reshape(in_weight.shape[0], -1), 'seq', axis=0,...  20.8 us
    all_to_all x2, starting transfers between devices, to_columns(): lax.all_to_all(signals, 'seq', split_axis=1, concat_axis=2, tiled=True)  19 us
    all_to_all x1, waiting for transfers between devices, to_rows(): lax.all_to_all(pieces, 'seq', split_axis=0, concat_axis=0, tiled=True)  13.7 us
    ppermute x8, starting transfers between devices, doubled_gather(): arrived = lax.ppermute(gathered, axis, route)  12.9 us
    all_to_all x1, starting transfers between devices, to_rows(): lax.all_to_all(pieces, 'seq', split_axis=0, concat_axis=0, tiled=True)  6.64 us
    all_to_all x2, waiting for transfers between devices, to_columns(): lax.all_to_all(signals, 'seq', split_axis=1, concat_axis=2, tiled=True)  6.49 us
  transfers between devices with their start and end apart: 15, of which 12 were waited for; matrix products, arithmetic and copies ran while one was open for 9% of the time, Pallas kernels for 0%

profile of v2, /device:TPU:2, one launch (start us, length us, event | category | flops | bytes accessed | tf_op | source)
XLA Modules:
  0.0 258.1 jit_solution(16284532907384214713)
XLA Ops:
  8.8 2.2 collective-permute-start.1
  12.6 11.0 %all-to-all-start.1 = ((f32[1,256,128]{2,0,1:T(1,128)}), f32[1,256,128]{2,0,1:T(1,128)S(1)}, u32[]{:S(2)}, u32[]{:S(2)}) async-start(f32[1,256,128]{2,0,1:T(1,128)} %bitcast.46), calls=%async_computation.1 | async-start | bytes 262144 | tf_op jit(solution)/shard_map/all_to_all | solution.py:53
  27.0 3.9 %collective-permute-done.2 = bf16[2,64,256]{2,1,0:T(8,128)(2,1)S(1)} collective-permute-done((bf16[2,64,256]{2,1,0:T(8,128)(2,1)S(1)}, bf16[2,64,256]{2,1,0:T(8,128)(2,1)S(1)}, u32[]{:S(2)}, u32[]{:S(2)}) %collective-permute-start.2) | collective-permute-done | bytes 65568 | tf_op jit(solution)/shard_map/ppermute | solution.py:26
  31.0 5.3 %collective-permute-start.3 = (bf16[2,2,64,256]{3,2,0,1:T(8,128)(2,1)S(1)}, bf16[2,2,64,256]{3,2,0,1:T(8,128)(2,1)S(1)}, u32[]{:S(2)}, u32[]{:S(2)}) collective-permute-start(bf16[2,2,64,256]{3,2,0,1:T(8,128)(2,1)S(1)} %maximum_select_fusion.7), channel_id=1, source_target_pairs={{0,32},{4,36},{8,40},{12,44},{16,48},{20,52},{24,56},{28,60},{32,0... | collective-permute-start | bytes 393224 | tf_op jit(solution)/shard_map/ppermute | solution.py:26
  36.4 6.3 %collective-permute-done.3 = bf16[2,2,64,256]{3,2,0,1:T(8,128)(2,1)S(1)} collective-permute-done((bf16[2,2,64,256]{3,2,0,1:T(8,128)(2,1)S(1)}, bf16[2,2,64,256]{3,2,0,1:T(8,128)(2,1)S(1)}, u32[]{:S(2)}, u32[]{:S(2)}) %collective-permute-start.3) | collective-permute-done | bytes 131104 | tf_op jit(solution)/shard_map/ppermute | solution.py:26
  42.7 3.0 %collective-permute-start.4 = (bf16[2,2,2,64,256]{4,3,0,1,2:T(8,128)(2,1)S(1)}, bf16[2,2,2,64,256]{4,3,0,1,2:T(8,128)(2,1)S(1)}, u32[]{:S(2)}, u32[]{:S(2)}) collective-permute-start(bf16[2,2,2,64,256]{4,3,0,1,2:T(8,128)(2,1)S(1)} %maximum_select_fusion.6), channel_id=1, source_target_pairs={{0,16},{4,20},{8,24},{12,28},{16,0},{20,4},{24,8},{28,12},{32,48},... | collective-permute-start | bytes 786440 | tf_op jit(solution)/shard_map/ppermute | solution.py:26
  45.8 11.4 %collective-permute-done.4 = bf16[2,2,2,64,256]{4,3,0,1,2:T(8,128)(2,1)S(1)} collective-permute-done((bf16[2,2,2,64,256]{4,3,0,1,2:T(8,128)(2,1)S(1)}, bf16[2,2,2,64,256]{4,3,0,1,2:T(8,128)(2,1)S(1)}, u32[]{:S(2)}, u32[]{:S(2)}) %collective-permute-start.4) | collective-permute-done | bytes 262176 | tf_op jit(solution)/shard_map/ppermute | solution.py:26
  58.1 13.6 %collective-permute-done.5 = bf16[2,2,2,2,64,256]{5,4,0,1,2,3:T(8,128)(2,1)S(1)} collective-permute-done((bf16[2,2,2,2,64,256]{5,4,0,1,2,3:T(8,128)(2,1)S(1)}, bf16[2,2,2,2,64,256]{5,4,0,1,2,3:T(8,128)(2,1)S(1)}, u32[]{:S(2)}, u32[]{:S(2)}) %collective-permute-start.5) | collective-permute-done | bytes 524320 | tf_op jit(solution)/shard_map/ppermute | solution.py:26
  76.4 1.9 maximum_select_fusion
  78.3 20.8 %all-gather.2.cloned.1.call-done = bf16[4096,768]{1,0:T(8,128)(2,1)} async-done(((bf16[64,768]{1,0:T(8,128)(2,1)}), bf16[4096,768]{1,0:T(8,128)(2,1)}) %all-gather.2.cloned.1.call-update) | async-done | bytes 6291472 | tf_op jit(solution)/shard_map/all_gather | solution.py:130
  99.1 3.9 %convolution_convert_fusion.1 = bf16[128,768]{1,0:T(8,128)(2,1)S(1)} fusion(bf16[4096,768]{1,0:T(8,128)(2,1)} %all-gather.2.cloned.1.call-done, bf16[128,4096]{1,0:T(8,128)(2,1)S(1)} %copy-done, f32[4096]{0:T(1024)} %param.9, f32[128]{0:T(128)S(1)} %get-tuple-element.42), kind=kOutput, calls=%fused_computation.15 | convolution fusion | flops 807501824 | bytes 7553536 | tf_op jit(solution)/shard_map/dot_general | solution.py:134
  104.3 2.1 collective-permute-start
  115.9 7.9 %all-to-all-start = ((f32[2,256,128]{2,0,1:T(2,128)}), f32[2,256,128]{2,0,1:T(2,128)}, u32[]{:S(2)}, u32[]{:S(2)}) async-start(f32[2,256,128]{2,0,1:T(2,128)} %copy.120), calls=%async_computation | async-start | bytes 524288 | tf_op jit(solution)/shard_map/all_to_all | solution.py:53
  125.4 2.2 fusion.3
  128.8 6.5 %all-to-all-done = f32[2,256,128]{2,0,1:T(2,128)} async-done(((f32[2,256,128]{2,0,1:T(2,128)}), f32[2,256,128]{2,0,1:T(2,128)}, u32[]{:S(2)}, u32[]{:S(2)}) %all-to-all-start) | async-done | bytes 262176 | tf_op jit(solution)/shard_map/all_to_all | solution.py:53
  148.4 6.6 %all-to-all-start.2 = ((f32[64,3,4,128]{3,2,1,0:T(4,128)}), f32[64,3,4,128]{3,2,1,0:T(4,128)}, u32[]{:S(2)}, u32[]{:S(2)}) async-start(f32[64,3,4,128]{3,2,1,0:T(4,128)} %copy.131), calls=%async_computation.2 | async-start | bytes 786432 | tf_op jit(solution)/shard_map/all_to_all | solution.py:61
  155.4 13.7 %all-to-all-done.2 = f32[64,3,4,128]{3,2,1,0:T(4,128)} async-done(((f32[64,3,4,128]{3,2,1,0:T(4,128)}), f32[64,3,4,128]{3,2,1,0:T(4,128)}, u32[]{:S(2)}, u32[]{:S(2)}) %all-to-all-start.2) | async-done | bytes 393248 | tf_op jit(solution)/shard_map/all_to_all | solution.py:61
  176.2 2.9 %collective-permute-start.7 = (f32[2,3,256]{2,0,1:T(2,128)S(1)}, f32[2,3,256]{2,0,1:T(2,128)S(1)}, u32[]{:S(2)}, u32[]{:S(2)}) collective-permute-start(f32[2,3,256]{2,0,1:T(2,128)S(1)} %slice.119), channel_id=1, source_target_pairs={{4,0},{8,4},{12,8},{16,12},{20,16},{24,20},{28,24},{32,28},{36,32}... | collective-permute-start | bytes 18440 | tf_op jit(solution)/shard_map/ppermute | solution.py:15
  179.1 1.8 convolution_convert_fusion
  181.7 5.0 %fusion.116 = (bf16[128,4096]{1,0:T(8,128)(2,1)S(1)}, f32[128]{0:T(128)S(1)}) fusion(bf16[128,4096]{1,0:T(8,128)(2,1)S(1)} %copy-done, f32[4096]{0:T(1024)S(1)} %copy-done.20, bf16[128,768]{0,1:T(8,128)(2,1)S(1)} %bitcast.260, bf16[4096,768]{1,0:T(8,128)(2,1)} %all-gather.2.cloned.1.call-done), kind=kOutput, calls=%fused_computation.190 | convolution fusion | flops 807927680 | bytes 8602112 | tf_op jit(solution)/shard_map/dot_general | solution.py:181
  191.8 31.6 %reduce-scatter.2.cloned.1.call-done = bf16[1,128,2176]{2,1,0:T(8,128)(2,1)} async-done(((bf16[4,128,2176]{2,1,0:T(8,128)(2,1)}), bf16[1,128,2176]{2,1,0:T(8,128)(2,1)}) %reduce-scatter.2.cloned.1.call-update) | async-done | bytes 557072 | tf_op jit(solution)/shard_map/reduce_scatter | solution.py:198
  224.7 1.9 fusion.20
  228.1 8.0 %collective-permute-done.8 = bf16[1,128,1024]{2,1,0:T(8,128)(2,1)S(1)} collective-permute-done((bf16[1,128,1024]{2,1,0:T(8,128)(2,1)S(1)}, bf16[1,128,1024]{2,1,0:T(8,128)(2,1)S(1)}, u32[]{:S(2)}, u32[]{:S(2)}) %collective-permute-start.8) | collective-permute-done | bytes 262176 | tf_op jit(solution)/shard_map/ppermute | solution.py:26
  237.4 11.6 %collective-permute-done.9 = bf16[2,1,128,1024]{3,2,1,0:T(8,128)(2,1)S(1)} collective-permute-done((bf16[2,1,128,1024]{3,2,1,0:T(8,128)(2,1)S(1)}, bf16[2,1,128,1024]{3,2,1,0:T(8,128)(2,1)S(1)}, u32[]{:S(2)}, u32[]{:S(2)}) %collective-permute-start.9) | collective-permute-done | bytes 524320 | tf_op jit(solution)/shard_map/ppermute | solution.py:26
  (153 shorter events, 57.9 us)
Async XLA Ops:
  7.2 19.3 %copy-start.18 = (bf16[256,64]{0,1:T(8,128)(2,1)S(1)}, bf16[256,64]{0,1:T(8,128)(2,1)}, u32[]{:S(2)}) copy-start(bf16[256,64]{0,1:T(8,128)(2,1)} %param.14) | copy-start | bytes 98308
  7.2 91.9 %all-gather.2.cloned.1.call-start = ((), (), s32[]{:S(2)}) async-start(), calls=%async_computation.4 | async-start | bytes 6389760 | tf_op jit(solution)/shard_map/all_gather | solution.py:130
  8.8 17.6 %collective-permute-start.1 = (bf16[64,256]{1,0:T(8,128)(2,1)}, bf16[64,256]{1,0:T(8,128)(2,1)S(1)}, u32[]{:S(2)}, u32[]{:S(2)}) collective-permute-start(bf16[64,256]{1,0:T(8,128)(2,1)} %bitcast.267), channel_id=1, source_target_pairs={{0,128},{4,132},{8,136},{12,140},{16,144},{20,148},{24,152},{28,15... | collective-permute-start | bytes 98312 | tf_op jit(solution)/shard_map/ppermute | solution.py:26
  12.6 61.6 %all-to-all-start.1 = ((f32[1,256,128]{2,0,1:T(1,128)}), f32[1,256,128]{2,0,1:T(1,128)S(1)}, u32[]{:S(2)}, u32[]{:S(2)}) async-start(f32[1,256,128]{2,0,1:T(1,128)} %bitcast.46), calls=%async_computation.1 | async-start | bytes 262144 | tf_op jit(solution)/shard_map/all_to_all | solution.py:53
  24.8 48.7 %copy-start.4 = (f32[128,128]{1,0:T(8,128)}, f32[128,128]{1,0:T(8,128)S(1)}, u32[]{:S(2)}) copy-start(f32[128,128]{1,0:T(8,128)S(1)} %get-tuple-element.37) | copy-start | bytes 196612
  26.4 4.5 %collective-permute-start.2 = (bf16[2,64,256]{2,1,0:T(8,128)(2,1)S(1)}, bf16[2,64,256]{2,1,0:T(8,128)(2,1)S(1)}, u32[]{:S(2)}, u32[]{:S(2)}) collective-permute-start(bf16[2,64,256]{2,1,0:T(8,128)(2,1)S(1)} %maximum_select_fusion.8), channel_id=1, source_target_pairs={{0,64},{4,68},{8,72},{12,76},{16,80},{20,84},{24,88},{28,92},{32,9... | collective-permute-start | bytes 196616 | tf_op jit(solution)/shard_map/ppermute | solution.py:26
  31.0 11.7 %collective-permute-start.3 = (bf16[2,2,64,256]{3,2,0,1:T(8,128)(2,1)S(1)}, bf16[2,2,64,256]{3,2,0,1:T(8,128)(2,1)S(1)}, u32[]{:S(2)}, u32[]{:S(2)}) collective-permute-start(bf16[2,2,64,256]{3,2,0,1:T(8,128)(2,1)S(1)} %maximum_select_fusion.7), channel_id=1, source_target_pairs={{0,32},{4,36},{8,40},{12,44},{16,48},{20,52},{24,56},{28,60},{32,0... | collective-permute-start | bytes 393224 | tf_op jit(solution)/shard_map/ppermute | solution.py:26
  42.7 14.5 %collective-permute-start.4 = (bf16[2,2,2,64,256]{4,3,0,1,2:T(8,128)(2,1)S(1)}, bf16[2,2,2,64,256]{4,3,0,1,2:T(8,128)(2,1)S(1)}, u32[]{:S(2)}, u32[]{:S(2)}) collective-permute-start(bf16[2,2,2,64,256]{4,3,0,1,2:T(8,128)(2,1)S(1)} %maximum_select_fusion.6), channel_id=1, source_target_pairs={{0,16},{4,20},{8,24},{12,28},{16,0},{20,4},{24,8},{28,12},{32,48},... | collective-permute-start | bytes 786440 | tf_op jit(solution)/shard_map/ppermute | solution.py:26
  57.3 14.4 %collective-permute-start.5 = (bf16[2,2,2,2,64,256]{5,4,0,1,2,3:T(8,128)(2,1)S(1)}, bf16[2,2,2,2,64,256]{5,4,0,1,2,3:T(8,128)(2,1)S(1)}, u32[]{:S(2)}, u32[]{:S(2)}) collective-permute-start(bf16[2,2,2,2,64,256]{5,4,0,1,2,3:T(8,128)(2,1)S(1)} %maximum_select_fusion.3), channel_id=1, source_target_pairs={{0,8},{4,12},{8,0},{12,4},{16,24},{20,28},{24,16},{28,20},{32,40},... | collective-permute-start | bytes 1572872 | tf_op jit(solution)/shard_map/ppermute | solution.py:26
  58.0 41.1 %copy-start.23 = (f32[128]{0:T(128)}, f32[128]{0:T(128)S(1)}, u32[]{:S(2)}) copy-start(f32[128]{0:T(128)S(1)} %get-tuple-element.42) | copy-start | bytes 1540
  72.8 3.6 %collective-permute-start.6 = (bf16[2,2,2,2,2,64,256]{6,5,0,1,2,3,4:T(8,128)(2,1)}, bf16[2,2,2,2,2,64,256]{6,5,0,1,2,3,4:T(8,128)(2,1)}, u32[]{:S(2)}, u32[]{:S(2)}) collective-permute-start(bf16[2,2,2,2,2,64,256]{6,5,0,1,2,3,4:T(8,128)(2,1)} %maximum_select_fusion.1), channel_id=1, source_target_pairs={{0,4},{4,0},{8,12},{12,8},{16,20},{20,16},{24,28},{28,24},{32,36},... | collective-permute-start | bytes 3145736 | tf_op jit(solution)/shard_map/ppermute | solution.py:26
  76.4 22.7 %copy-start = (bf16[128,4096]{1,0:T(8,128)(2,1)S(1)}, bf16[128,4096]{1,0:T(8,128)(2,1)}, u32[]{:S(2)}) copy-start(bf16[128,4096]{1,0:T(8,128)(2,1)} %param.8) | copy-start | bytes 3145732
  104.3 7.2 %collective-permute-start = (bf16[2,3,256]{2,0,1:T(2,128)(2,1)}, bf16[2,3,256]{2,0,1:T(2,128)(2,1)S(1)}, u32[]{:S(2)}, u32[]{:S(2)}) collective-permute-start(bf16[2,3,256]{2,0,1:T(2,128)(2,1)} %bitcast), channel_id=1, source_target_pairs={{0,4},{4,8},{8,12},{12,16},{16,20},{20,24},{24,28},{28,32},{32,36}... | collective-permute-start | bytes 9224 | tf_op jit(solution)/shard_map/ppermute | solution.py:15
  115.9 19.4 %all-to-all-start = ((f32[2,256,128]{2,0,1:T(2,128)}), f32[2,256,128]{2,0,1:T(2,128)}, u32[]{:S(2)}, u32[]{:S(2)}) async-start(f32[2,256,128]{2,0,1:T(2,128)} %copy.120), calls=%async_computation | async-start | bytes 524288 | tf_op jit(solution)/shard_map/all_to_all | solution.py:53
  147.3 26.7 %copy-start.13 = (f32[128,256]{1,0:T(8,128)S(1)}, f32[128,256]{1,0:T(8,128)}, u32[]{:S(2)}) copy-start(f32[128,256]{1,0:T(8,128)} %convolution_bitcast_fusion.2) | copy-start | bytes 393220
  147.4 26.7 %copy-start.21 = (f32[256]{0:T(256)S(1)}, f32[256]{0:T(256)}, u32[]{:S(2)}) copy-start(f32[256]{0:T(256)} %param.13) | copy-start | bytes 3076
  148.4 20.7 %all-to-all-start.2 = ((f32[64,3,4,128]{3,2,1,0:T(4,128)}), f32[64,3,4,128]{3,2,1,0:T(4,128)}, u32[]{:S(2)}, u32[]{:S(2)}) async-start(f32[64,3,4,128]{3,2,1,0:T(4,128)} %copy.131), calls=%async_computation.2 | async-start | bytes 786432 | tf_op jit(solution)/shard_map/all_to_all | solution.py:61
  155.0 68.4 %reduce-scatter.2.cloned.1.call-start = ((), (), s32[]{:S(2)}) async-start(), calls=%async_computation.5 | async-start | bytes 2785280 | tf_op jit(solution)/shard_map/reduce_scatter | solution.py:198
  176.2 4.8 %collective-permute-start.7 = (f32[2,3,256]{2,0,1:T(2,128)S(1)}, f32[2,3,256]{2,0,1:T(2,128)S(1)}, u32[]{:S(2)}, u32[]{:S(2)}) collective-permute-start(f32[2,3,256]{2,0,1:T(2,128)S(1)} %slice.119), channel_id=1, source_target_pairs={{4,0},{8,4},{12,8},{16,12},{20,16},{24,20},{28,24},{32,28},{36,32}... | collective-permute-start | bytes 18440 | tf_op jit(solution)/shard_map/ppermute | solution.py:15
  191.5 33.2 %copy-start.22 = (f32[128]{0:T(128)S(1)}, f32[128]{0:T(128)}, u32[]{:S(2)}) copy-start(f32[128]{0:T(128)} %get-tuple-element.41) | copy-start | bytes 1540
  191.6 33.2 %copy-start.24 = (f32[128]{0:T(128)S(1)}, f32[128]{0:T(128)}, u32[]{:S(2)}) copy-start(f32[128]{0:T(128)} %copy-done.23) | copy-start | bytes 1540
  224.5 12.0 %copy-start.17 = (f32[1,128,64,4]{1,3,0,2:T(4,128)S(1)}, f32[1,128,64,4]{1,3,0,2:T(4,128)}, u32[]{:S(2)}) copy-start(f32[1,128,64,4]{1,3,0,2:T(4,128)} %get-tuple-element.29) | copy-start | bytes 393220
  226.7 9.5 %collective-permute-start.8 = (bf16[1,128,1024]{2,1,0:T(8,128)(2,1)S(1)}, bf16[1,128,1024]{2,1,0:T(8,128)(2,1)S(1)}, u32[]{:S(2)}, u32[]{:S(2)}) collective-permute-start(bf16[1,128,1024]{2,1,0:T(8,128)(2,1)S(1)} %bitcast.245), channel_id=1, source_target_pairs={{0,2},{1,3},{2,0},{3,1},{4,6},{5,7},{6,4},{7,5},{8,10},{9,11},{10,... | collective-permute-start | bytes 786440 | tf_op jit(solution)/shard_map/ppermute | solution.py:26
  236.2 12.8 %collective-permute-start.9 = (bf16[2,1,128,1024]{3,2,1,0:T(8,128)(2,1)S(1)}, bf16[2,1,128,1024]{3,2,1,0:T(8,128)(2,1)S(1)}, u32[]{:S(2)}, u32[]{:S(2)}) collective-permute-start(bf16[2,1,128,1024]{3,2,1,0:T(8,128)(2,1)S(1)} %maximum_select_fusion.5), channel_id=1, source_target_pairs={{0,1},{1,0},{2,3},{3,2},{4,5},{5,4},{6,7},{7,6},{8,9},{9,8},{10,11... | collective-permute-start | bytes 1572872 | tf_op jit(solution)/shard_map/ppermute | solution.py:26
  (16 other events, 47.1 us)
Sparse Core Ops, SparseCore 0:
  10.7 88.3 all-gather.1
  191.7 31.6 reduce-scatter.1

commit v3 on v2

--- a/solution.py
+++ b/solution.py
@@ -88,24 +88,23 @@
     turned_real = first_real * cos_tw + first_imag * sin_tw
     turned_imag = first_imag * cos_tw - first_real * sin_tw
     cos_in, sin_in = turn_table(inner, inner, inner, 1.0)
-    spec_real = jnp.einsum("uckm,mj->uckj", turned_real, cos_in, precision=lax.Precision.HIGH) + jnp.einsum(
-        "uckm,mj->uckj", turned_imag, sin_in, precision=lax.Precision.HIGH
-    )
-    spec_imag = jnp.einsum("uckm,mj->uckj", turned_imag, cos_in, precision=lax.Precision.HIGH) - jnp.einsum(
-        "uckm,mj->uckj", turned_real, sin_in, precision=lax.Precision.HIGH
-    )
-    return spec_real, spec_imag
+    rotation = jnp.concatenate(
+        [jnp.concatenate([cos_in, -sin_in], 1), jnp.concatenate([sin_in, cos_in], 1)], 0
+    )
+    joined = jnp.concatenate([turned_real, turned_imag], -1)
+    spec = jnp.einsum("uckm,mj->uckj", joined, rotation, precision=lax.Precision.HIGH)
+    return spec[..., :inner], spec[..., inner:]
 
 
 def inverse_dft(spec_real, spec_imag):
     count, chans, outer, inner = spec_real.shape
     cos_in, sin_in = turn_table(inner, inner, inner, 1.0)
-    back_real = jnp.einsum("uckj,jm->uckm", spec_real, cos_in, precision=lax.Precision.HIGH) - jnp.einsum(
-        "uckj,jm->uckm", spec_imag, sin_in, precision=lax.Precision.HIGH
-    )
-    back_imag = jnp.einsum("uckj,jm->uckm", spec_imag, cos_in, precision=lax.Precision.HIGH) + jnp.einsum(
-        "uckj,jm->uckm", spec_real, sin_in, precision=lax.Precision.HIGH
-    )
+    rotation = jnp.concatenate(
+        [jnp.concatenate([cos_in, sin_in], 1), jnp.concatenate([-sin_in, cos_in], 1)], 0
+    )
+    joined = jnp.concatenate([spec_real, spec_imag], -1)
+    back = jnp.einsum("uckj,jm->uckm", joined, rotation, precision=lax.Precision.HIGH)
+    back_real, back_imag = back[..., :inner], back[..., inner:]
     cos_tw, sin_tw = turn_table(outer, inner, outer * inner, 1.0)
     turned_real = back_real * cos_tw - back_imag * sin_tw
     turned_imag = back_imag * cos_tw + back_real * sin_tw

time: 259 us -> 252 us (0.973)
  matrix products: 30.3 us -> 22.1 us
    dot_general x12 -> x3, matrix products: 12.5 us -> 4.15 us  [the longest x2 3.36 us: forward_dft(): jnp.einsum('uckm,mj->uckj', joined, rotation, precision=lax.Precision.HIGH)]
    all_to_all x2, waiting for transfers between devices: 6.49 us -> 1.22 us  [to_columns(): lax.all_to_all(signals, 'seq', split_axis=1, concat_axis=2, tiled=True)]
    ppermute x8, waiting for transfers between devices: 55.2 us -> 60.3 us  [doubled_gather(): arrived = lax.ppermute(gathered, axis, route)]
    ppermute x2, waiting for transfers between devices: 0.44 us -> 4.01 us  [passed_along(): return lax.ppermute(block, axis, route)]
    all_to_all x1, starting transfers between devices: 6.64 us -> 9.29 us  [to_rows(): lax.all_to_all(pieces, 'seq', split_axis=0, concat_axis=0, tiled=True)]
    unnamed x55 -> x43, local copies, waits for them, and re-layouts: 5.49 us -> 3.86 us
  transfers between devices with their start and end apart: 15 -> 15, of which waited for: 12 -> 13; matrix products, arithmetic and copies ran while one was open for 9% -> 12% of each run, Pallas kernels for 0% -> 0%
where the time goes in v3:
time: 252 us; the launch traced here: 251 us
  waiting for transfers between devices  129 us (51%)
  starting transfers between devices  45.6 us (18%)
  local copies, waits for them, and re-layouts  22.7 us (9%)
  matrix products  22.1 us (9%)
  other arithmetic  17.2 us (7%)
  between operations  14.7 us (6%)
    ppermute x8, waiting for transfers between devices, doubled_gather(): arrived = lax.ppermute(gathered, axis, route)  60.3 us
    reduce_scatter x1, waiting for transfers between devices, per_device(): lax.psum_scatter(payload, 'ch', scatter_dimension=0).astype(jnp.float32)  31.7 us
    all_gather x1, waiting for transfers between devices, per_device(): lax.all_gather(in_weight.reshape(in_weight.shape[0], -1), 'seq', axis=0,...  18.2 us
    all_to_all x2, starting transfers between devices, to_columns(): lax.all_to_all(signals, 'seq', split_axis=1, concat_axis=2, tiled=True)  18 us
    all_to_all x1, waiting for transfers between devices, to_rows(): lax.all_to_all(pieces, 'seq', split_axis=0, concat_axis=0, tiled=True)  13.3 us
    ppermute x8, starting transfers between devices, doubled_gather(): arrived = lax.ppermute(gathered, axis, route)  13.2 us
    all_to_all x1, starting transfers between devices, to_rows(): lax.all_to_all(pieces, 'seq', split_axis=0, concat_axis=0, tiled=True)  9.29 us
  transfers between devices with their start and end apart: 15, of which 13 were waited for; matrix products, arithmetic and copies ran while one was open for 12% of the time, Pallas kernels for 0%

profile of v3, /device:TPU:2, one launch (start us, length us, event | category | flops | bytes accessed | tf_op | source)
XLA Modules:
  0.0 251.1 jit_solution(12353109774143118556)
XLA Ops:
  8.8 2.2 collective-permute-start.1
  12.6 11.2 %all-to-all-start.1 = ((f32[1,256,128]{2,0,1:T(1,128)}), f32[1,256,128]{2,0,1:T(1,128)}, u32[]{:S(2)}, u32[]{:S(2)}) async-start(f32[1,256,128]{2,0,1:T(1,128)} %bitcast.1), calls=%async_computation.1 | async-start | bytes 262144 | tf_op jit(solution)/shard_map/all_to_all | solution.py:53
  27.9 2.9 %collective-permute-done.2 = bf16[2,64,256]{2,1,0:T(8,128)(2,1)S(1)} collective-permute-done((bf16[2,64,256]{2,1,0:T(8,128)(2,1)S(1)}, bf16[2,64,256]{2,1,0:T(8,128)(2,1)S(1)}, u32[]{:S(2)}, u32[]{:S(2)}) %collective-permute-start.2) | collective-permute-done | bytes 65568 | tf_op jit(solution)/shard_map/ppermute | solution.py:26
  30.8 5.0 %collective-permute-start.3 = (bf16[2,2,64,256]{3,2,0,1:T(8,128)(2,1)S(1)}, bf16[2,2,64,256]{3,2,0,1:T(8,128)(2,1)S(1)}, u32[]{:S(2)}, u32[]{:S(2)}) collective-permute-start(bf16[2,2,64,256]{3,2,0,1:T(8,128)(2,1)S(1)} %maximum_select_fusion.7), channel_id=1, source_target_pairs={{0,32},{4,36},{8,40},{12,44},{16,48},{20,52},{24,56},{28,60},{32,0... | collective-permute-start | bytes 393224 | tf_op jit(solution)/shard_map/ppermute | solution.py:26
  35.9 6.8 %collective-permute-done.3 = bf16[2,2,64,256]{3,2,0,1:T(8,128)(2,1)S(1)} collective-permute-done((bf16[2,2,64,256]{3,2,0,1:T(8,128)(2,1)S(1)}, bf16[2,2,64,256]{3,2,0,1:T(8,128)(2,1)S(1)}, u32[]{:S(2)}, u32[]{:S(2)}) %collective-permute-start.3) | collective-permute-done | bytes 131104 | tf_op jit(solution)/shard_map/ppermute | solution.py:26
  42.8 3.4 %collective-permute-start.4 = (bf16[2,2,2,64,256]{4,3,0,1,2:T(8,128)(2,1)S(1)}, bf16[2,2,2,64,256]{4,3,0,1,2:T(8,128)(2,1)S(1)}, u32[]{:S(2)}, u32[]{:S(2)}) collective-permute-start(bf16[2,2,2,64,256]{4,3,0,1,2:T(8,128)(2,1)S(1)} %maximum_select_fusion.6), channel_id=1, source_target_pairs={{0,16},{4,20},{8,24},{12,28},{16,0},{20,4},{24,8},{28,12},{32,48},... | collective-permute-start | bytes 786440 | tf_op jit(solution)/shard_map/ppermute | solution.py:26
  46.2 13.2 %collective-permute-done.4 = bf16[2,2,2,64,256]{4,3,0,1,2:T(8,128)(2,1)S(1)} collective-permute-done((bf16[2,2,2,64,256]{4,3,0,1,2:T(8,128)(2,1)S(1)}, bf16[2,2,2,64,256]{4,3,0,1,2:T(8,128)(2,1)S(1)}, u32[]{:S(2)}, u32[]{:S(2)}) %collective-permute-start.4) | collective-permute-done | bytes 262176 | tf_op jit(solution)/shard_map/ppermute | solution.py:26
  61.0 16.1 %collective-permute-done.5 = bf16[2,2,2,2,64,256]{5,4,0,1,2,3:T(8,128)(2,1)S(1)} collective-permute-done((bf16[2,2,2,2,64,256]{5,4,0,1,2,3:T(8,128)(2,1)S(1)}, bf16[2,2,2,2,64,256]{5,4,0,1,2,3:T(8,128)(2,1)S(1)}, u32[]{:S(2)}, u32[]{:S(2)}) %collective-permute-start.5) | collective-permute-done | bytes 524320 | tf_op jit(solution)/shard_map/ppermute | solution.py:26
  80.3 18.2 %all-gather.2.cloned.1.call-done = bf16[4096,768]{1,0:T(8,128)(2,1)} async-done(((bf16[64,768]{1,0:T(8,128)(2,1)}), bf16[4096,768]{1,0:T(8,128)(2,1)}) %all-gather.2.cloned.1.call-update) | async-done | bytes 6291472 | tf_op jit(solution)/shard_map/all_gather | solution.py:129
  98.5 3.9 %convolution_convert_fusion.1 = bf16[128,768]{1,0:T(8,128)(2,1)S(1)} fusion(bf16[4096,768]{1,0:T(8,128)(2,1)} %all-gather.2.cloned.1.call-done, bf16[128,4096]{1,0:T(8,128)(2,1)S(1)} %copy-done, f32[4096]{0:T(1024)S(1)} %copy-done.12, f32[128]{0:T(128)S(1)} %get-tuple-element.49), kind=kOutput, calls=%fused_computation.24 | convolution fusion | flops 807501824 | bytes 7553536 | tf_op jit(solution)/shard_map/dot_general | solution.py:133
  103.0 2.1 collective-permute-start
  106.6 3.6 %collective-permute-done = bf16[2,3,256]{2,0,1:T(2,128)(2,1)S(1)} collective-permute-done((bf16[2,3,256]{2,0,1:T(2,128)(2,1)}, bf16[2,3,256]{2,0,1:T(2,128)(2,1)S(1)}, u32[]{:S(2)}, u32[]{:S(2)}) %collective-permute-start) | collective-permute-done | bytes 3104 | tf_op jit(solution)/shard_map/ppermute | solution.py:15
  111.2 1.8 copy.120
  113.0 6.8 %all-to-all-start = ((f32[2,256,128]{2,0,1:T(2,128)}), f32[2,256,128]{2,0,1:T(2,128)}, u32[]{:S(2)}, u32[]{:S(2)}) async-start(f32[2,256,128]{2,0,1:T(2,128)} %copy.120), calls=%async_computation | async-start | bytes 524288 | tf_op jit(solution)/shard_map/all_to_all | solution.py:53
  119.8 2.0 fusion.111
  127.7 2.3 convolution_bitcast_fusion
  138.8 9.3 %all-to-all-start.2 = ((f32[64,3,4,128]{3,2,1,0:T(4,128)}), f32[64,3,4,128]{3,2,1,0:T(4,128)}, u32[]{:S(2)}, u32[]{:S(2)}) async-start(f32[64,3,4,128]{3,2,1,0:T(4,128)} %copy.131), calls=%async_computation.2 | async-start | bytes 786432 | tf_op jit(solution)/shard_map/all_to_all | solution.py:61
  148.8 13.3 %all-to-all-done.2 = f32[64,3,4,128]{3,2,1,0:T(4,128)} async-done(((f32[64,3,4,128]{3,2,1,0:T(4,128)}), f32[64,3,4,128]{3,2,1,0:T(4,128)}, u32[]{:S(2)}, u32[]{:S(2)}) %all-to-all-start.2) | async-done | bytes 393248 | tf_op jit(solution)/shard_map/all_to_all | solution.py:61
  170.0 2.9 %collective-permute-start.7 = (f32[2,3,256]{2,0,1:T(2,128)S(1)}, f32[2,3,256]{2,0,1:T(2,128)S(1)}, u32[]{:S(2)}, u32[]{:S(2)}) collective-permute-start(f32[2,3,256]{2,0,1:T(2,128)S(1)} %slice.145), channel_id=1, source_target_pairs={{4,0},{8,4},{12,8},{16,12},{20,16},{24,20},{28,24},{32,28},{36,32}... | collective-permute-start | bytes 18440 | tf_op jit(solution)/shard_map/ppermute | solution.py:15
  174.6 5.0 %fusion.112 = (bf16[128,4096]{1,0:T(8,128)(2,1)S(1)}, f32[128]{0:T(128)S(1)}) fusion(bf16[128,4096]{1,0:T(8,128)(2,1)S(1)} %copy-done, f32[4096]{0:T(1024)S(1)} %copy-done.13, bf16[128,768]{0,1:T(8,128)(2,1)S(1)} %bitcast.237, bf16[4096,768]{1,0:T(8,128)(2,1)} %all-gather.2.cloned.1.call-done), kind=kOutput, calls=%fused_computation.193 | convolution fusion | flops 807927680 | bytes 8602112 | tf_op jit(solution)/shard_map/dot_general | solution.py:180
  184.7 31.7 %reduce-scatter.2.cloned.1.call-done = bf16[1,128,2176]{2,1,0:T(8,128)(2,1)} async-done(((bf16[4,128,2176]{2,1,0:T(8,128)(2,1)}), bf16[1,128,2176]{2,1,0:T(8,128)(2,1)}) %reduce-scatter.2.cloned.1.call-update) | async-done | bytes 557072 | tf_op jit(solution)/shard_map/reduce_scatter | solution.py:197
  217.7 1.9 fusion.36
  221.1 8.0 %collective-permute-done.8 = bf16[1,128,1024]{2,1,0:T(8,128)(2,1)S(1)} collective-permute-done((bf16[1,128,1024]{2,1,0:T(8,128)(2,1)S(1)}, bf16[1,128,1024]{2,1,0:T(8,128)(2,1)S(1)}, u32[]{:S(2)}, u32[]{:S(2)}) %collective-permute-start.8) | collective-permute-done | bytes 262176 | tf_op jit(solution)/shard_map/ppermute | solution.py:26
  230.4 11.7 %collective-permute-done.9 = bf16[2,1,128,1024]{3,2,1,0:T(8,128)(2,1)S(1)} collective-permute-done((bf16[2,1,128,1024]{3,2,1,0:T(8,128)(2,1)S(1)}, bf16[2,1,128,1024]{3,2,1,0:T(8,128)(2,1)S(1)}, u32[]{:S(2)}, u32[]{:S(2)}) %collective-permute-start.9) | collective-permute-done | bytes 524320 | tf_op jit(solution)/shard_map/ppermute | solution.py:26
  (134 shorter events, 50.9 us)
Async XLA Ops:
  7.2 91.3 %all-gather.2.cloned.1.call-start = ((), (), s32[]{:S(2)}) async-start(), calls=%async_computation.4 | async-start | bytes 6389760 | tf_op jit(solution)/shard_map/all_gather | solution.py:129
  8.8 16.0 %collective-permute-start.1 = (bf16[64,256]{1,0:T(8,128)(2,1)}, bf16[64,256]{1,0:T(8,128)(2,1)S(1)}, u32[]{:S(2)}, u32[]{:S(2)}) collective-permute-start(bf16[64,256]{1,0:T(8,128)(2,1)} %bitcast.244), channel_id=1, source_target_pairs={{0,128},{4,132},{8,136},{12,140},{16,144},{20,148},{24,152},{28,15... | collective-permute-start | bytes 98312 | tf_op jit(solution)/shard_map/ppermute | solution.py:26
  12.6 100.4 %all-to-all-start.1 = ((f32[1,256,128]{2,0,1:T(1,128)}), f32[1,256,128]{2,0,1:T(1,128)}, u32[]{:S(2)}, u32[]{:S(2)}) async-start(f32[1,256,128]{2,0,1:T(1,128)} %bitcast.1), calls=%async_computation.1 | async-start | bytes 262144 | tf_op jit(solution)/shard_map/all_to_all | solution.py:53
  25.6 5.2 %collective-permute-start.2 = (bf16[2,64,256]{2,1,0:T(8,128)(2,1)S(1)}, bf16[2,64,256]{2,1,0:T(8,128)(2,1)S(1)}, u32[]{:S(2)}, u32[]{:S(2)}) collective-permute-start(bf16[2,64,256]{2,1,0:T(8,128)(2,1)S(1)} %maximum_select_fusion.8), channel_id=1, source_target_pairs={{0,64},{4,68},{8,72},{12,76},{16,80},{20,84},{24,88},{28,92},{32,9... | collective-permute-start | bytes 196616 | tf_op jit(solution)/shard_map/ppermute | solution.py:26
  30.8 11.9 %collective-permute-start.3 = (bf16[2,2,64,256]{3,2,0,1:T(8,128)(2,1)S(1)}, bf16[2,2,64,256]{3,2,0,1:T(8,128)(2,1)S(1)}, u32[]{:S(2)}, u32[]{:S(2)}) collective-permute-start(bf16[2,2,64,256]{3,2,0,1:T(8,128)(2,1)S(1)} %maximum_select_fusion.7), channel_id=1, source_target_pairs={{0,32},{4,36},{8,40},{12,44},{16,48},{20,52},{24,56},{28,60},{32,0... | collective-permute-start | bytes 393224 | tf_op jit(solution)/shard_map/ppermute | solution.py:26
  42.8 16.7 %collective-permute-start.4 = (bf16[2,2,2,64,256]{4,3,0,1,2:T(8,128)(2,1)S(1)}, bf16[2,2,2,64,256]{4,3,0,1,2:T(8,128)(2,1)S(1)}, u32[]{:S(2)}, u32[]{:S(2)}) collective-permute-start(bf16[2,2,2,64,256]{4,3,0,1,2:T(8,128)(2,1)S(1)} %maximum_select_fusion.6), channel_id=1, source_target_pairs={{0,16},{4,20},{8,24},{12,28},{16,0},{20,4},{24,8},{28,12},{32,48},... | collective-permute-start | bytes 786440 | tf_op jit(solution)/shard_map/ppermute | solution.py:26
  59.5 17.6 %collective-permute-start.5 = (bf16[2,2,2,2,64,256]{5,4,0,1,2,3:T(8,128)(2,1)S(1)}, bf16[2,2,2,2,64,256]{5,4,0,1,2,3:T(8,128)(2,1)S(1)}, u32[]{:S(2)}, u32[]{:S(2)}) collective-permute-start(bf16[2,2,2,2,64,256]{5,4,0,1,2,3:T(8,128)(2,1)S(1)} %maximum_select_fusion.3), channel_id=1, source_target_pairs={{0,8},{4,12},{8,0},{12,4},{16,24},{20,28},{24,16},{28,20},{32,40},... | collective-permute-start | bytes 1572872 | tf_op jit(solution)/shard_map/ppermute | solution.py:26
  60.9 16.4 %copy-start = (bf16[128,4096]{1,0:T(8,128)(2,1)S(1)}, bf16[128,4096]{1,0:T(8,128)(2,1)}, u32[]{:S(2)}) copy-start(bf16[128,4096]{1,0:T(8,128)(2,1)} %param.8) | copy-start | bytes 3145732
  77.2 2.9 %collective-permute-start.6 = (bf16[2,2,2,2,2,64,256]{6,5,0,1,2,3,4:T(8,128)(2,1)S(1)}, bf16[2,2,2,2,2,64,256]{6,5,0,1,2,3,4:T(8,128)(2,1)S(1)}, u32[]{:S(2)}, u32[]{:S(2)}) collective-permute-start(bf16[2,2,2,2,2,64,256]{6,5,0,1,2,3,4:T(8,128)(2,1)S(1)} %maximum_select_fusion.1), channel_id=1, source_target_pairs={{0,4},{4,0},{8,12},{12,8},{16,20},{20,16},{24,28},{28,24},{32,36},... | collective-permute-start | bytes 3145736 | tf_op jit(solution)/shard_map/ppermute | solution.py:26
  78.2 20.3 %copy-start.17 = (f32[128]{0:T(128)}, f32[128]{0:T(128)S(1)}, u32[]{:S(2)}) copy-start(f32[128]{0:T(128)S(1)} %get-tuple-element.49) | copy-start | bytes 1540
  80.1 18.4 %copy-start.12 = (f32[4096]{0:T(1024)S(1)}, f32[4096]{0:T(1024)}, u32[]{:S(2)}) copy-start(f32[4096]{0:T(1024)} %param.9) | copy-start | bytes 49156
  98.5 6.6 %copy-start.2 = (bf16[128,4096]{1,0:T(8,128)(2,1)S(1)}, bf16[128,4096]{1,0:T(8,128)(2,1)}, u32[]{:S(2)}) copy-start(bf16[128,4096]{1,0:T(8,128)(2,1)} %param.15) | copy-start | bytes 3145732
  103.0 7.2 %collective-permute-start = (bf16[2,3,256]{2,0,1:T(2,128)(2,1)}, bf16[2,3,256]{2,0,1:T(2,128)(2,1)S(1)}, u32[]{:S(2)}, u32[]{:S(2)}) collective-permute-start(bf16[2,3,256]{2,0,1:T(2,128)(2,1)} %bitcast.8), channel_id=1, source_target_pairs={{0,4},{4,8},{8,12},{12,16},{16,20},{20,24},{24,28},{28,32},{32,36}... | collective-permute-start | bytes 9224 | tf_op jit(solution)/shard_map/ppermute | solution.py:15
  113.0 18.2 %all-to-all-start = ((f32[2,256,128]{2,0,1:T(2,128)}), f32[2,256,128]{2,0,1:T(2,128)}, u32[]{:S(2)}, u32[]{:S(2)}) async-start(f32[2,256,128]{2,0,1:T(2,128)} %copy.120), calls=%async_computation | async-start | bytes 524288 | tf_op jit(solution)/shard_map/all_to_all | solution.py:53
  137.3 31.6 %copy-start.14 = (f32[256]{0:T(256)S(1)}, f32[256]{0:T(256)}, u32[]{:S(2)}) copy-start(f32[256]{0:T(256)} %param.13) | copy-start | bytes 3076
  138.8 23.3 %all-to-all-start.2 = ((f32[64,3,4,128]{3,2,1,0:T(4,128)}), f32[64,3,4,128]{3,2,1,0:T(4,128)}, u32[]{:S(2)}, u32[]{:S(2)}) async-start(f32[64,3,4,128]{3,2,1,0:T(4,128)} %copy.131), calls=%async_computation.2 | async-start | bytes 786432 | tf_op jit(solution)/shard_map/all_to_all | solution.py:61
  148.1 68.3 %reduce-scatter.2.cloned.1.call-start = ((), (), s32[]{:S(2)}) async-start(), calls=%async_computation.5 | async-start | bytes 2785280 | tf_op jit(solution)/shard_map/reduce_scatter | solution.py:197
  168.8 4.1 %copy-start.10 = (f32[128,1,256]{2,0,1:T(8,128)S(1)}, f32[128,1,256]{2,0,1:T(8,128)}, u32[]{:S(2)}) copy-start(f32[128,1,256]{2,0,1:T(8,128)} %copy.132) | copy-start | bytes 393220
  170.0 4.2 %collective-permute-start.7 = (f32[2,3,256]{2,0,1:T(2,128)S(1)}, f32[2,3,256]{2,0,1:T(2,128)S(1)}, u32[]{:S(2)}, u32[]{:S(2)}) collective-permute-start(f32[2,3,256]{2,0,1:T(2,128)S(1)} %slice.145), channel_id=1, source_target_pairs={{4,0},{8,4},{12,8},{16,12},{20,16},{24,20},{28,24},{32,28},{36,32}... | collective-permute-start | bytes 18440 | tf_op jit(solution)/shard_map/ppermute | solution.py:15
  184.4 33.3 %copy-start.16 = (f32[128]{0:T(128)S(1)}, f32[128]{0:T(128)}, u32[]{:S(2)}) copy-start(f32[128]{0:T(128)} %get-tuple-element.48) | copy-start | bytes 1540
  184.4 33.3 %copy-start.18 = (f32[128]{0:T(128)S(1)}, f32[128]{0:T(128)}, u32[]{:S(2)}) copy-start(f32[128]{0:T(128)} %copy-done.17) | copy-start | bytes 1540
  217.5 12.0 %copy-start.11 = (f32[1,128,64,4]{1,3,0,2:T(4,128)S(1)}, f32[1,128,64,4]{1,3,0,2:T(4,128)}, u32[]{:S(2)}) copy-start(f32[1,128,64,4]{1,3,0,2:T(4,128)} %get-tuple-element.33) | copy-start | bytes 393220
  219.7 9.5 %collective-permute-start.8 = (bf16[1,128,1024]{2,1,0:T(8,128)(2,1)S(1)}, bf16[1,128,1024]{2,1,0:T(8,128)(2,1)S(1)}, u32[]{:S(2)}, u32[]{:S(2)}) collective-permute-start(bf16[1,128,1024]{2,1,0:T(8,128)(2,1)S(1)} %bitcast.223), channel_id=1, source_target_pairs={{0,2},{1,3},{2,0},{3,1},{4,6},{5,7},{6,4},{7,5},{8,10},{9,11},{10,... | collective-permute-start | bytes 786440 | tf_op jit(solution)/shard_map/ppermute | solution.py:26
  229.2 12.8 %collective-permute-start.9 = (bf16[2,1,128,1024]{3,2,1,0:T(8,128)(2,1)S(1)}, bf16[2,1,128,1024]{3,2,1,0:T(8,128)(2,1)S(1)}, u32[]{:S(2)}, u32[]{:S(2)}) collective-permute-start(bf16[2,1,128,1024]{3,2,1,0:T(8,128)(2,1)S(1)} %maximum_select_fusion.5), channel_id=1, source_target_pairs={{0,1},{1,0},{2,3},{3,2},{4,5},{5,4},{6,7},{7,6},{8,9},{9,8},{10,11... | collective-permute-start | bytes 1572872 | tf_op jit(solution)/shard_map/ppermute | solution.py:26
  (10 other events, 21.4 us)
Sparse Core Ops, SparseCore 0:
  11.3 87.1 all-gather.1
  184.5 31.7 reduce-scatter.1

commit v4 on v3

--- a/solution.py
+++ b/solution.py
@@ -82,8 +82,10 @@
     outer, inner = fft_sizes(seq_total)
     grid = signals.reshape(count, chans, outer // 2, inner)
     cos_out, sin_out = turn_table(outer, outer // 2, outer, 1.0)
-    first_real = jnp.einsum("kn,ucnm->uckm", cos_out, grid, precision=lax.Precision.HIGH)
-    first_imag = -jnp.einsum("kn,ucnm->uckm", sin_out, grid, precision=lax.Precision.HIGH)
+    first = jnp.einsum(
+        "kn,ucnm->uckm", jnp.concatenate([cos_out, -sin_out], 0), grid, precision=lax.Precision.HIGH
+    )
+    first_real, first_imag = first[:, :, :outer], first[:, :, outer:]
     cos_tw, sin_tw = turn_table(outer, inner, outer * inner, 1.0)
     turned_real = first_real * cos_tw + first_imag * sin_tw
     turned_imag = first_imag * cos_tw - first_real * sin_tw
@@ -109,8 +111,11 @@
     turned_real = back_real * cos_tw - back_imag * sin_tw
     turned_imag = back_imag * cos_tw + back_real * sin_tw
     cos_out, sin_out = turn_table(outer, outer // 2, outer, 1.0)
-    grid = jnp.einsum("kn,uckm->ucnm", cos_out, turned_real, precision=lax.Precision.HIGH) - jnp.einsum(
-        "kn,uckm->ucnm", sin_out, turned_imag, precision=lax.Precision.HIGH
+    grid = jnp.einsum(
+        "kn,uckm->ucnm",
+        jnp.concatenate([cos_out, -sin_out], 0),
+        jnp.concatenate([turned_real, turned_imag], 2),
+        precision=lax.Precision.HIGH,
     )
     return grid.reshape(count, chans, outer * inner // 2) / float(outer * inner)
 

time: 252 us -> 251 us (level)
  matrix products: 22.1 us -> 18.6 us
  waiting for transfers between devices: 129 us -> 132 us
  starting transfers between devices: 45.6 us -> 42.9 us
    ppermute x8, waiting for transfers between devices: 60.3 us -> 52.5 us  [doubled_gather(): arrived = lax.ppermute(gathered, axis, route)]
    all_gather x1, waiting for transfers between devices: 18.2 us -> 25 us  [per_device(): lax.all_gather(in_weight.reshape(in_weight.shape[0], -1), 'seq', axis=0,...]
    all_to_all x2, waiting for transfers between devices: 1.22 us -> 5.28 us  [to_columns(): lax.all_to_all(signals, 'seq', split_axis=1, concat_axis=2, tiled=True)]
    dot_general x6 -> x3, matrix products: 7.05 us -> 3.58 us  [the longest x2 2.95 us: forward_dft(): jnp.einsum('kn,ucnm->uckm', jnp.concatenate([cos_out, -sin_out], 0), grid...]
    all_to_all x1, starting transfers between devices: 9.29 us -> 6.64 us  [to_rows(): lax.all_to_all(pieces, 'seq', split_axis=0, concat_axis=0, tiled=True)]
  transfers between devices with their start and end apart: 15 -> 15, of which waited for: 13 -> 13; matrix products, arithmetic and copies ran while one was open for 12% -> 11% of each run, Pallas kernels for 0% -> 0%
where the time goes in v4:
time: 251 us; the launch traced here: 249 us
  waiting for transfers between devices  132 us (53%)
  starting transfers between devices  42.9 us (17%)
  local copies, waits for them, and re-layouts  22.1 us (9%)
  other arithmetic  18.8 us (7%)
  matrix products  18.6 us (7%)
  between operations  14.7 us (6%)
    ppermute x8, waiting for transfers between devices, doubled_gather(): arrived = lax.ppermute(gathered, axis, route)  52.5 us
    reduce_scatter x1, waiting for transfers between devices, per_device(): lax.psum_scatter(payload, 'ch', scatter_dimension=0).astype(jnp.float32)  32 us
    all_gather x1, waiting for transfers between devices, per_device(): lax.all_gather(in_weight.reshape(in_weight.shape[0], -1), 'seq', axis=0,...  25 us
    all_to_all x2, starting transfers between devices, to_columns(): lax.all_to_all(signals, 'seq', split_axis=1, concat_axis=2, tiled=True)  17.7 us
    ppermute x8, starting transfers between devices, doubled_gather(): arrived = lax.ppermute(gathered, axis, route)  13.5 us
    all_to_all x1, waiting for transfers between devices, to_rows(): lax.all_to_all(pieces, 'seq', split_axis=0, concat_axis=0, tiled=True)  13.4 us
    all_to_all x1, starting transfers between devices, to_rows(): lax.all_to_all(pieces, 'seq', split_axis=0, concat_axis=0, tiled=True)  6.64 us
    all_to_all x2, waiting for transfers between devices, to_columns(): lax.all_to_all(signals, 'seq', split_axis=1, concat_axis=2, tiled=True)  5.28 us
  transfers between devices with their start and end apart: 15, of which 13 were waited for; matrix products, arithmetic and copies ran while one was open for 11% of the time, Pallas kernels for 0%

profile of v4, /device:TPU:2, one launch (start us, length us, event | category | flops | bytes accessed | tf_op | source)
XLA Modules:
  0.0 249.4 jit_solution(18105231908628929155)
XLA Ops:
  8.8 2.2 collective-permute-start.1
  12.6 11.2 %all-to-all-start.1 = ((f32[1,256,128]{2,0,1:T(1,128)}), f32[1,256,128]{2,0,1:T(1,128)}, u32[]{:S(2)}, u32[]{:S(2)}) async-start(f32[1,256,128]{2,0,1:T(1,128)} %bitcast.1), calls=%async_computation.1 | async-start | bytes 262144 | tf_op jit(solution)/shard_map/all_to_all | solution.py:53
  28.5 2.5 %collective-permute-done.2 = bf16[2,64,256]{2,1,0:T(8,128)(2,1)S(1)} collective-permute-done((bf16[2,64,256]{2,1,0:T(8,128)(2,1)S(1)}, bf16[2,64,256]{2,1,0:T(8,128)(2,1)S(1)}, u32[]{:S(2)}, u32[]{:S(2)}) %collective-permute-start.2) | collective-permute-done | bytes 65568 | tf_op jit(solution)/shard_map/ppermute | solution.py:26
  31.0 5.2 %collective-permute-start.3 = (bf16[2,2,64,256]{3,2,0,1:T(8,128)(2,1)S(1)}, bf16[2,2,64,256]{3,2,0,1:T(8,128)(2,1)S(1)}, u32[]{:S(2)}, u32[]{:S(2)}) collective-permute-start(bf16[2,2,64,256]{3,2,0,1:T(8,128)(2,1)S(1)} %maximum_select_fusion.7), channel_id=1, source_target_pairs={{0,32},{4,36},{8,40},{12,44},{16,48},{20,52},{24,56},{28,60},{32,0... | collective-permute-start | bytes 393224 | tf_op jit(solution)/shard_map/ppermute | solution.py:26
  36.3 6.4 %collective-permute-done.3 = bf16[2,2,64,256]{3,2,0,1:T(8,128)(2,1)S(1)} collective-permute-done((bf16[2,2,64,256]{3,2,0,1:T(8,128)(2,1)S(1)}, bf16[2,2,64,256]{3,2,0,1:T(8,128)(2,1)S(1)}, u32[]{:S(2)}, u32[]{:S(2)}) %collective-permute-start.3) | collective-permute-done | bytes 131104 | tf_op jit(solution)/shard_map/ppermute | solution.py:26
  42.7 3.4 %collective-permute-start.4 = (bf16[2,2,2,64,256]{4,3,0,1,2:T(8,128)(2,1)S(1)}, bf16[2,2,2,64,256]{4,3,0,1,2:T(8,128)(2,1)S(1)}, u32[]{:S(2)}, u32[]{:S(2)}) collective-permute-start(bf16[2,2,2,64,256]{4,3,0,1,2:T(8,128)(2,1)S(1)} %maximum_select_fusion.6), channel_id=1, source_target_pairs={{0,16},{4,20},{8,24},{12,28},{16,0},{20,4},{24,8},{28,12},{32,48},... | collective-permute-start | bytes 786440 | tf_op jit(solution)/shard_map/ppermute | solution.py:26
  46.3 11.2 %collective-permute-done.4 = bf16[2,2,2,64,256]{4,3,0,1,2:T(8,128)(2,1)S(1)} collective-permute-done((bf16[2,2,2,64,256]{4,3,0,1,2:T(8,128)(2,1)S(1)}, bf16[2,2,2,64,256]{4,3,0,1,2:T(8,128)(2,1)S(1)}, u32[]{:S(2)}, u32[]{:S(2)}) %collective-permute-start.4) | collective-permute-done | bytes 262176 | tf_op jit(solution)/shard_map/ppermute | solution.py:26
  60.3 11.2 %collective-permute-done.5 = bf16[2,2,2,2,64,256]{5,4,0,1,2,3:T(8,128)(2,1)S(1)} collective-permute-done((bf16[2,2,2,2,64,256]{5,4,0,1,2,3:T(8,128)(2,1)S(1)}, bf16[2,2,2,2,64,256]{5,4,0,1,2,3:T(8,128)(2,1)S(1)}, u32[]{:S(2)}, u32[]{:S(2)}) %collective-permute-start.5) | collective-permute-done | bytes 524320 | tf_op jit(solution)/shard_map/ppermute | solution.py:26
  74.6 25.0 %all-gather.2.cloned.1.call-done = bf16[4096,768]{1,0:T(8,128)(2,1)} async-done(((bf16[64,768]{1,0:T(8,128)(2,1)}), bf16[4096,768]{1,0:T(8,128)(2,1)}) %all-gather.2.cloned.1.call-update) | async-done | bytes 6291472 | tf_op jit(solution)/shard_map/all_gather | solution.py:134
  99.6 3.9 %convolution_convert_fusion.1 = bf16[128,768]{1,0:T(8,128)(2,1)S(1)} fusion(bf16[4096,768]{1,0:T(8,128)(2,1)} %all-gather.2.cloned.1.call-done, bf16[128,4096]{1,0:T(8,128)(2,1)S(1)} %copy-done, f32[4096]{0:T(1024)S(1)} %copy-done.17, f32[128]{0:T(128)S(1)} %get-tuple-element.53), kind=kOutput, calls=%fused_computation.26 | convolution fusion | flops 807501824 | bytes 7553536 | tf_op jit(solution)/shard_map/dot_general | solution.py:138
  104.1 2.1 collective-permute-start
  107.8 3.6 %collective-permute-done = bf16[2,3,256]{2,0,1:T(2,128)(2,1)S(1)} collective-permute-done((bf16[2,3,256]{2,0,1:T(2,128)(2,1)}, bf16[2,3,256]{2,0,1:T(2,128)(2,1)S(1)}, u32[]{:S(2)}, u32[]{:S(2)}) %collective-permute-start) | collective-permute-done | bytes 3104 | tf_op jit(solution)/shard_map/ppermute | solution.py:15
  112.3 1.8 copy.120
  114.1 6.5 %all-to-all-start = ((f32[2,256,128]{2,0,1:T(2,128)}), f32[2,256,128]{2,0,1:T(2,128)}, u32[]{:S(2)}, u32[]{:S(2)}) async-start(f32[2,256,128]{2,0,1:T(2,128)} %copy.120), calls=%async_computation | async-start | bytes 524288 | tf_op jit(solution)/shard_map/all_to_all | solution.py:53
  124.4 2.3 convolution_bitcast_fusion.1
  126.8 5.3 %all-to-all-done = f32[2,256,128]{2,0,1:T(2,128)} async-done(((f32[2,256,128]{2,0,1:T(2,128)}), f32[2,256,128]{2,0,1:T(2,128)}, u32[]{:S(2)}, u32[]{:S(2)}) %all-to-all-start) | async-done | bytes 262176 | tf_op jit(solution)/shard_map/all_to_all | solution.py:53
  139.3 6.6 %all-to-all-start.2 = ((f32[64,3,4,128]{3,2,1,0:T(4,128)}), f32[64,3,4,128]{3,2,1,0:T(4,128)}, u32[]{:S(2)}, u32[]{:S(2)}) async-start(f32[64,3,4,128]{3,2,1,0:T(4,128)} %copy.131), calls=%async_computation.2 | async-start | bytes 786432 | tf_op jit(solution)/shard_map/all_to_all | solution.py:61
  146.6 13.4 %all-to-all-done.2 = f32[64,3,4,128]{3,2,1,0:T(4,128)} async-done(((f32[64,3,4,128]{3,2,1,0:T(4,128)}), f32[64,3,4,128]{3,2,1,0:T(4,128)}, u32[]{:S(2)}, u32[]{:S(2)}) %all-to-all-start.2) | async-done | bytes 393248 | tf_op jit(solution)/shard_map/all_to_all | solution.py:61
  167.9 2.9 %collective-permute-start.7 = (f32[2,3,256]{2,0,1:T(2,128)S(1)}, f32[2,3,256]{2,0,1:T(2,128)S(1)}, u32[]{:S(2)}, u32[]{:S(2)}) collective-permute-start(f32[2,3,256]{2,0,1:T(2,128)S(1)} %slice.165), channel_id=1, source_target_pairs={{4,0},{8,4},{12,8},{16,12},{20,16},{24,20},{28,24},{32,28},{36,32}... | collective-permute-start | bytes 18440 | tf_op jit(solution)/shard_map/ppermute | solution.py:15
  172.5 5.0 %fusion.90 = (bf16[128,4096]{1,0:T(8,128)(2,1)S(1)}, f32[128]{0:T(128)S(1)}) fusion(bf16[128,4096]{1,0:T(8,128)(2,1)S(1)} %copy-done, f32[4096]{0:T(1024)S(1)} %copy-done.18, bf16[128,768]{0,1:T(8,128)(2,1)S(1)} %bitcast.206, bf16[4096,768]{1,0:T(8,128)(2,1)} %all-gather.2.cloned.1.call-done), kind=kOutput, calls=%fused_computation.176 | convolution fusion | flops 807927680 | bytes 8602112 | tf_op jit(solution)/shard_map/dot_general | solution.py:185
  182.6 32.0 %reduce-scatter.2.cloned.1.call-done = bf16[1,128,2176]{2,1,0:T(8,128)(2,1)} async-done(((bf16[4,128,2176]{2,1,0:T(8,128)(2,1)}), bf16[1,128,2176]{2,1,0:T(8,128)(2,1)}) %reduce-scatter.2.cloned.1.call-update) | async-done | bytes 557072 | tf_op jit(solution)/shard_map/reduce_scatter | solution.py:202
  216.0 1.9 fusion.29
  219.3 8.0 %collective-permute-done.8 = bf16[1,128,1024]{2,1,0:T(8,128)(2,1)S(1)} collective-permute-done((bf16[1,128,1024]{2,1,0:T(8,128)(2,1)S(1)}, bf16[1,128,1024]{2,1,0:T(8,128)(2,1)S(1)}, u32[]{:S(2)}, u32[]{:S(2)}) %collective-permute-start.8) | collective-permute-done | bytes 262176 | tf_op jit(solution)/shard_map/ppermute | solution.py:26
  228.6 11.7 %collective-permute-done.9 = bf16[2,1,128,1024]{3,2,1,0:T(8,128)(2,1)S(1)} collective-permute-done((bf16[2,1,128,1024]{3,2,1,0:T(8,128)(2,1)S(1)}, bf16[2,1,128,1024]{3,2,1,0:T(8,128)(2,1)S(1)}, u32[]{:S(2)}, u32[]{:S(2)}) %collective-permute-start.9) | collective-permute-done | bytes 524320 | tf_op jit(solution)/shard_map/ppermute | solution.py:26
  (145 shorter events, 49.2 us)
Async XLA Ops:
  7.2 92.5 %all-gather.2.cloned.1.call-start = ((), (), s32[]{:S(2)}) async-start(), calls=%async_computation.4 | async-start | bytes 6389760 | tf_op jit(solution)/shard_map/all_gather | solution.py:134
  8.8 16.6 %collective-permute-start.1 = (bf16[64,256]{1,0:T(8,128)(2,1)}, bf16[64,256]{1,0:T(8,128)(2,1)S(1)}, u32[]{:S(2)}, u32[]{:S(2)}) collective-permute-start(bf16[64,256]{1,0:T(8,128)(2,1)} %bitcast.213), channel_id=1, source_target_pairs={{0,128},{4,132},{8,136},{12,140},{16,144},{20,148},{24,152},{28,15... | collective-permute-start | bytes 98312 | tf_op jit(solution)/shard_map/ppermute | solution.py:26
  12.6 101.5 %all-to-all-start.1 = ((f32[1,256,128]{2,0,1:T(1,128)}), f32[1,256,128]{2,0,1:T(1,128)}, u32[]{:S(2)}, u32[]{:S(2)}) async-start(f32[1,256,128]{2,0,1:T(1,128)} %bitcast.1), calls=%async_computation.1 | async-start | bytes 262144 | tf_op jit(solution)/shard_map/all_to_all | solution.py:53
  26.2 4.8 %collective-permute-start.2 = (bf16[2,64,256]{2,1,0:T(8,128)(2,1)S(1)}, bf16[2,64,256]{2,1,0:T(8,128)(2,1)S(1)}, u32[]{:S(2)}, u32[]{:S(2)}) collective-permute-start(bf16[2,64,256]{2,1,0:T(8,128)(2,1)S(1)} %maximum_select_fusion.8), channel_id=1, source_target_pairs={{0,64},{4,68},{8,72},{12,76},{16,80},{20,84},{24,88},{28,92},{32,9... | collective-permute-start | bytes 196616 | tf_op jit(solution)/shard_map/ppermute | solution.py:26
  31.0 11.7 %collective-permute-start.3 = (bf16[2,2,64,256]{3,2,0,1:T(8,128)(2,1)S(1)}, bf16[2,2,64,256]{3,2,0,1:T(8,128)(2,1)S(1)}, u32[]{:S(2)}, u32[]{:S(2)}) collective-permute-start(bf16[2,2,64,256]{3,2,0,1:T(8,128)(2,1)S(1)} %maximum_select_fusion.7), channel_id=1, source_target_pairs={{0,32},{4,36},{8,40},{12,44},{16,48},{20,52},{24,56},{28,60},{32,0... | collective-permute-start | bytes 393224 | tf_op jit(solution)/shard_map/ppermute | solution.py:26
  42.7 14.7 %collective-permute-start.4 = (bf16[2,2,2,64,256]{4,3,0,1,2:T(8,128)(2,1)S(1)}, bf16[2,2,2,64,256]{4,3,0,1,2:T(8,128)(2,1)S(1)}, u32[]{:S(2)}, u32[]{:S(2)}) collective-permute-start(bf16[2,2,2,64,256]{4,3,0,1,2:T(8,128)(2,1)S(1)} %maximum_select_fusion.6), channel_id=1, source_target_pairs={{0,16},{4,20},{8,24},{12,28},{16,0},{20,4},{24,8},{28,12},{32,48},... | collective-permute-start | bytes 786440 | tf_op jit(solution)/shard_map/ppermute | solution.py:26
  57.5 14.0 %collective-permute-start.5 = (bf16[2,2,2,2,64,256]{5,4,0,1,2,3:T(8,128)(2,1)S(1)}, bf16[2,2,2,2,64,256]{5,4,0,1,2,3:T(8,128)(2,1)S(1)}, u32[]{:S(2)}, u32[]{:S(2)}) collective-permute-start(bf16[2,2,2,2,64,256]{5,4,0,1,2,3:T(8,128)(2,1)S(1)} %maximum_select_fusion.3), channel_id=1, source_target_pairs={{0,8},{4,12},{8,0},{12,4},{16,24},{20,28},{24,16},{28,20},{32,40},... | collective-permute-start | bytes 1572872 | tf_op jit(solution)/shard_map/ppermute | solution.py:26
  60.3 11.5 %copy-start = (bf16[128,4096]{1,0:T(8,128)(2,1)S(1)}, bf16[128,4096]{1,0:T(8,128)(2,1)}, u32[]{:S(2)}) copy-start(bf16[128,4096]{1,0:T(8,128)(2,1)} %param.8) | copy-start | bytes 3145732
  71.7 2.8 %collective-permute-start.6 = (bf16[2,2,2,2,2,64,256]{6,5,0,1,2,3,4:T(8,128)(2,1)S(1)}, bf16[2,2,2,2,2,64,256]{6,5,0,1,2,3,4:T(8,128)(2,1)S(1)}, u32[]{:S(2)}, u32[]{:S(2)}) collective-permute-start(bf16[2,2,2,2,2,64,256]{6,5,0,1,2,3,4:T(8,128)(2,1)S(1)} %maximum_select_fusion.1), channel_id=1, source_target_pairs={{0,4},{4,0},{8,12},{12,8},{16,20},{20,16},{24,28},{28,24},{32,36},... | collective-permute-start | bytes 3145736 | tf_op jit(solution)/shard_map/ppermute | solution.py:26
  72.6 27.0 %copy-start.22 = (f32[128]{0:T(128)}, f32[128]{0:T(128)S(1)}, u32[]{:S(2)}) copy-start(f32[128]{0:T(128)S(1)} %get-tuple-element.53) | copy-start | bytes 1540
  74.4 25.2 %copy-start.17 = (f32[4096]{0:T(1024)S(1)}, f32[4096]{0:T(1024)}, u32[]{:S(2)}) copy-start(f32[4096]{0:T(1024)} %param.9) | copy-start | bytes 49156
  99.6 6.6 %copy-start.2 = (bf16[128,4096]{1,0:T(8,128)(2,1)S(1)}, bf16[128,4096]{1,0:T(8,128)(2,1)}, u32[]{:S(2)}) copy-start(bf16[128,4096]{1,0:T(8,128)(2,1)} %param.15) | copy-start | bytes 3145732
  104.1 7.2 %collective-permute-start = (bf16[2,3,256]{2,0,1:T(2,128)(2,1)}, bf16[2,3,256]{2,0,1:T(2,128)(2,1)S(1)}, u32[]{:S(2)}, u32[]{:S(2)}) collective-permute-start(bf16[2,3,256]{2,0,1:T(2,128)(2,1)} %bitcast.6), channel_id=1, source_target_pairs={{0,4},{4,8},{8,12},{12,16},{16,20},{20,24},{24,28},{28,32},{32,36}... | collective-permute-start | bytes 9224 | tf_op jit(solution)/shard_map/ppermute | solution.py:15
  114.1 17.9 %all-to-all-start = ((f32[2,256,128]{2,0,1:T(2,128)}), f32[2,256,128]{2,0,1:T(2,128)}, u32[]{:S(2)}, u32[]{:S(2)}) async-start(f32[2,256,128]{2,0,1:T(2,128)} %copy.120), calls=%async_computation | async-start | bytes 524288 | tf_op jit(solution)/shard_map/all_to_all | solution.py:53
  137.6 29.1 %copy-start.19 = (f32[256]{0:T(256)S(1)}, f32[256]{0:T(256)}, u32[]{:S(2)}) copy-start(f32[256]{0:T(256)} %param.13) | copy-start | bytes 3076
  139.3 20.7 %all-to-all-start.2 = ((f32[64,3,4,128]{3,2,1,0:T(4,128)}), f32[64,3,4,128]{3,2,1,0:T(4,128)}, u32[]{:S(2)}, u32[]{:S(2)}) async-start(f32[64,3,4,128]{3,2,1,0:T(4,128)} %copy.131), calls=%async_computation.2 | async-start | bytes 786432 | tf_op jit(solution)/shard_map/all_to_all | solution.py:61
  145.9 68.7 %reduce-scatter.2.cloned.1.call-start = ((), (), s32[]{:S(2)}) async-start(), calls=%async_computation.5 | async-start | bytes 2785280 | tf_op jit(solution)/shard_map/reduce_scatter | solution.py:202
  166.7 4.1 %copy-start.15 = (f32[128,1,256]{2,0,1:T(8,128)S(1)}, f32[128,1,256]{2,0,1:T(8,128)}, u32[]{:S(2)}) copy-start(f32[128,1,256]{2,0,1:T(8,128)} %copy.132) | copy-start | bytes 393220
  167.9 4.2 %collective-permute-start.7 = (f32[2,3,256]{2,0,1:T(2,128)S(1)}, f32[2,3,256]{2,0,1:T(2,128)S(1)}, u32[]{:S(2)}, u32[]{:S(2)}) collective-permute-start(f32[2,3,256]{2,0,1:T(2,128)S(1)} %slice.165), channel_id=1, source_target_pairs={{4,0},{8,4},{12,8},{16,12},{20,16},{24,20},{28,24},{32,28},{36,32}... | collective-permute-start | bytes 18440 | tf_op jit(solution)/shard_map/ppermute | solution.py:15
  182.3 33.6 %copy-start.21 = (f32[128]{0:T(128)S(1)}, f32[128]{0:T(128)}, u32[]{:S(2)}) copy-start(f32[128]{0:T(128)} %get-tuple-element.52) | copy-start | bytes 1540
  182.4 33.6 %copy-start.23 = (f32[128]{0:T(128)S(1)}, f32[128]{0:T(128)}, u32[]{:S(2)}) copy-start(f32[128]{0:T(128)} %copy-done.22) | copy-start | bytes 1540
  215.8 12.0 %copy-start.16 = (f32[1,128,64,4]{1,3,0,2:T(4,128)S(1)}, f32[1,128,64,4]{1,3,0,2:T(4,128)}, u32[]{:S(2)}) copy-start(f32[1,128,64,4]{1,3,0,2:T(4,128)} %get-tuple-element.35) | copy-start | bytes 393220
  217.9 9.5 %collective-permute-start.8 = (bf16[1,128,1024]{2,1,0:T(8,128)(2,1)S(1)}, bf16[1,128,1024]{2,1,0:T(8,128)(2,1)S(1)}, u32[]{:S(2)}, u32[]{:S(2)}) collective-permute-start(bf16[1,128,1024]{2,1,0:T(8,128)(2,1)S(1)} %bitcast.192), channel_id=1, source_target_pairs={{0,2},{1,3},{2,0},{3,1},{4,6},{5,7},{6,4},{7,5},{8,10},{9,11},{10,... | collective-permute-start | bytes 786440 | tf_op jit(solution)/shard_map/ppermute | solution.py:26
  227.5 12.8 %collective-permute-start.9 = (bf16[2,1,128,1024]{3,2,1,0:T(8,128)(2,1)S(1)}, bf16[2,1,128,1024]{3,2,1,0:T(8,128)(2,1)S(1)}, u32[]{:S(2)}, u32[]{:S(2)}) collective-permute-start(bf16[2,1,128,1024]{3,2,1,0:T(8,128)(2,1)S(1)} %maximum_select_fusion.5), channel_id=1, source_target_pairs={{0,1},{1,0},{2,3},{3,2},{4,5},{5,4},{6,7},{7,6},{8,9},{9,8},{10,11... | collective-permute-start | bytes 1572872 | tf_op jit(solution)/shard_map/ppermute | solution.py:26
  (15 other events, 24.3 us)
Sparse Core Ops, SparseCore 0:
  11.3 88.2 all-gather.1
  182.5 32.1 reduce-scatter.1
